TPU v7x, 32 devices: a whole 2x2x4 slice. The times are simulated.
32 devices in a mesh: dp: 8 (over y, x, core), tensor: 4 (over z).
Axes of the slice: x: 2, y: 2, z: 4, core: 2. Of those that a mesh axis runs over, the one named last changes fastest.
Arguments:
- tokens: bfloat16 [24576, 768], P(('dp', 'tensor')), may hold values from -6 to 6
- lengths: int32 [40], replicated, may hold values from 257 to 1024, as said below
- dealing: int32 [40], replicated, may hold values from 0 to 39, as said below
- w_query: bfloat16 [768, 768], P('dp', 'tensor'), may hold values from -0.4375 to 0.4375
- w_key: bfloat16 [768, 768], P('dp', 'tensor'), may hold values from -0.21875 to 0.21875
- w_value: bfloat16 [768, 768], P('dp', 'tensor'), may hold values from -0.21875 to 0.21875
- w_out: bfloat16 [768, 768], P('tensor', 'dp'), may hold values from -1.75 to 1.75
- w_inner: bfloat16 [768, 3072], P('dp', 'tensor'), may hold values from -0.21875 to 0.21875
- w_outer: bfloat16 [3072, 768], P('tensor', 'dp'), may hold values from -0.109375 to 0.109375
- b_query: bfloat16 [768], replicated, may hold values from -3 to 3
- b_value: bfloat16 [768], replicated, may hold values from -3 to 3
- b_out: bfloat16 [768], replicated, may hold values from -3 to 3
- b_inner: bfloat16 [3072], replicated, may hold values from -3 to 3
- b_outer: bfloat16 [768], replicated, may hold values from -3 to 3
- gain_attn: bfloat16 [768], replicated, may hold values from 0.5 to 1.5
- shift_attn: bfloat16 [768], replicated, may hold values from -2 to 2
- gain_ffn: bfloat16 [768], replicated, may hold values from 0.5 to 1.5
- shift_ffn: bfloat16 [768], replicated, may hold values from -2 to 2
- grad_out: bfloat16 [24576, 768], P(('dp', 'tensor')), may hold values from -6 to 6
Outputs:
- layer_out: bfloat16 [24576, 768], P(('dp', 'tensor'))
- grad_tokens: float32 [24576, 768], P(('dp', 'tensor'))
- grad_w_query: float32 [768, 768], P('dp', 'tensor')
- grad_w_key: float32 [768, 768], P('dp', 'tensor')
- grad_w_value: float32 [768, 768], P('dp', 'tensor')
- grad_w_out: float32 [768, 768], P('tensor', 'dp')
- grad_w_inner: float32 [768, 3072], P('dp', 'tensor')
- grad_w_outer: float32 [3072, 768], P('tensor', 'dp')
- grad_b_query: float32 [768], P(('dp', 'tensor'))
- grad_b_value: float32 [768], P(('dp', 'tensor'))
- grad_b_out: float32 [768], P(('dp', 'tensor'))
- grad_b_inner: float32 [3072], P(('dp', 'tensor'))
- grad_b_outer: float32 [768], P(('dp', 'tensor'))
- grad_gain_attn: float32 [768], P(('dp', 'tensor'))
- grad_shift_attn: float32 [768], P(('dp', 'tensor'))
- grad_gain_ffn: float32 [768], P(('dp', 'tensor'))
- grad_shift_ffn: float32 [768], P(('dp', 'tensor'))
Inputs may be any that keep to these rules, and one draw needn't show every extreme that they name: In every data group one dealt sequence has exactly 1024 tokens, and the lengths of the 5 sequences dealt to a group sum to 3072. `dealing`: A permutation of the sequences.
All inputs are finite; a program needn't handle non-finite values.
Results may differ from a plain program's by a relative error of at most 0.02.
Values may be sent and summed in bfloat16 or wider, within the bound.
No kernel may reach another device: no remote copies, remote signals or barrier semaphores. Data moves between devices by JAX's collectives and lax.ppermute only.
A program may use at most 128 MiB of HBM per device.

v0:
```python
import math

import jax
import jax.numpy as jnp
from jax import lax
from jax.experimental import pallas as pl
from jax.experimental.pallas import tpu as pltpu
from jax.sharding import PartitionSpec as P

HEAD_DIM = 64
LONGEST = 1024
BLOCK = 256

NEG = -1e30
LANES = 128


def _lanes(rows):
    return lax.broadcasted_iota(jnp.int32, (rows, LANES), 1) < LANES // 2


def _pick(first, second, lanes):
    return jnp.where(lanes, first, second)


def _nt(a, b):
    return lax.dot_general(a, b, (((1,), (1,)), ((), ())), preferred_element_type=jnp.float32)


def _tn(a, b):
    return lax.dot_general(a, b, (((0,), (0,)), ((), ())), preferred_element_type=jnp.float32)


def _nn(a, b):
    return lax.dot_general(a, b, (((1,), (0,)), ((), ())), preferred_element_type=jnp.float32)


def _attn_fwd(lo_ref, hi_ref, q_ref, k_ref, v_ref, qs_ref, ks_ref, o_ref, lse_ref, m_sc, l_sc, acc_sc):
    i = pl.program_id(0)
    j = pl.program_id(1)
    kv = lo_ref[i] + j
    pairs = q_ref.shape[1] // LANES
    bq = q_ref.shape[0]

    @pl.when(j == 0)
    def _():
        m_sc[...] = jnp.full_like(m_sc, NEG)
        l_sc[...] = jnp.zeros_like(l_sc)
        acc_sc[...] = jnp.zeros_like(acc_sc)

    @pl.when(kv <= hi_ref[i])
    def _():
        mask = qs_ref[...] == ks_ref[...]
        lanes = _lanes(bq)

        def pair(p, carry):
            cols = pl.ds(p * LANES, LANES)
            q2 = q_ref[:, cols]
            k2 = k_ref[:, cols]
            v2 = v_ref[:, cols]
            zero = jnp.zeros_like(q2)
            alphas, pvs = [], []
            for h in range(2):
                hq = _pick(q2, zero, lanes) if h == 0 else _pick(zero, q2, lanes)
                s = jnp.where(mask, _nt(hq, k2), NEG)
                m_old = m_sc[2 * p + h]
                m_new = jnp.maximum(m_old, jnp.max(s, axis=-1, keepdims=True))
                alpha = jnp.exp(m_old - m_new)
                e = jnp.exp(s - m_new)
                l_sc[2 * p + h] = alpha * l_sc[2 * p + h] + jnp.sum(e, axis=-1, keepdims=True)
                m_sc[2 * p + h] = m_new
                alphas.append(alpha)
                pvs.append(_nn(e.astype(jnp.bfloat16), v2))
            acc_sc[:, cols] = _pick(alphas[0], alphas[1], lanes) * acc_sc[:, cols] + _pick(pvs[0], pvs[1], lanes)
            return carry

        for p in range(pairs):
            pair(p, 0)

    @pl.when(j == pl.num_programs(1) - 1)
    def _():
        lanes = _lanes(bq)

        def pair(p, carry):
            cols = pl.ds(p * LANES, LANES)
            l0, l1 = l_sc[2 * p], l_sc[2 * p + 1]
            o_ref[:, cols] = acc_sc[:, cols] / _pick(l0, l1, lanes)
            lse_ref[2 * p] = m_sc[2 * p] + jnp.log(l0)
            lse_ref[2 * p + 1] = m_sc[2 * p + 1] + jnp.log(l1)
            return carry

        for p in range(pairs):
            pair(p, 0)


def _attn_dq(lo_ref, hi_ref, q_ref, k_ref, v_ref, qs_ref, ks_ref, lse_ref, dl_ref, do_ref, dq_ref, acc_sc):
    i = pl.program_id(0)
    j = pl.program_id(1)
    kv = lo_ref[i] + j
    pairs = q_ref.shape[1] // LANES
    bq = q_ref.shape[0]

    @pl.when(j == 0)
    def _():
        acc_sc[...] = jnp.zeros_like(acc_sc)

    @pl.when(kv <= hi_ref[i])
    def _():
        mask = qs_ref[...] == ks_ref[...]
        lanes = _lanes(bq)

        def pair(p, carry):
            cols = pl.ds(p * LANES, LANES)
            q2 = q_ref[:, cols]
            k2 = k_ref[:, cols]
            v2 = v_ref[:, cols]
            do2 = do_ref[:, cols]
            zero = jnp.zeros_like(q2)
            parts = []
            for h in range(2):
                sel = (lambda a: _pick(a, zero, lanes)) if h == 0 else (lambda a: _pick(zero, a, lanes))
                s = _nt(sel(q2), k2)
                e = jnp.where(mask, jnp.exp(s - lse_ref[2 * p + h]), 0.0)
                dp = _nt(sel(do2), v2)
                ds = (e * (dp - dl_ref[2 * p + h])).astype(jnp.bfloat16)
                parts.append(_nn(ds, k2))
            acc_sc[:, cols] += _pick(parts[0], parts[1], lanes)
            return carry

        for p in range(pairs):
            pair(p, 0)

    @pl.when(j == pl.num_programs(1) - 1)
    def _():
        dq_ref[...] = acc_sc[...] * 0.125


def _attn_dkv(lo_ref, hi_ref, q_ref, k_ref, v_ref, qs_ref, ks_ref, lse_ref, dl_ref, do_ref, dk_ref, dv_ref, dk_sc, dv_sc):
    j = pl.program_id(0)
    i = pl.program_id(1)
    qb = lo_ref[j] + i
    pairs = q_ref.shape[1] // LANES
    bq = q_ref.shape[0]
    bk = k_ref.shape[0]

    @pl.when(i == 0)
    def _():
        dk_sc[...] = jnp.zeros_like(dk_sc)
        dv_sc[...] = jnp.zeros_like(dv_sc)

    @pl.when(qb <= hi_ref[j])
    def _():
        mask = qs_ref[...] == ks_ref[...]
        lanes_q = _lanes(bq)
        lanes_k = _lanes(bk)

        def pair(p, carry):
            cols = pl.ds(p * LANES, LANES)
            q2 = q_ref[:, cols]
            k2 = k_ref[:, cols]
            v2 = v_ref[:, cols]
            do2 = do_ref[:, cols]
            zero = jnp.zeros_like(q2)
            dks, dvs = [], []
            for h in range(2):
                sel = (lambda a: _pick(a, zero, lanes_q)) if h == 0 else (lambda a: _pick(zero, a, lanes_q))
                s = _nt(sel(q2), k2)
                e = jnp.where(mask, jnp.exp(s - lse_ref[2 * p + h]), 0.0)
                dp = _nt(sel(do2), v2)
                ds = (e * (dp - dl_ref[2 * p + h])).astype(jnp.bfloat16)
                dvs.append(_tn(e.astype(jnp.bfloat16), do2))
                dks.append(_tn(ds, q2))
            dv_sc[:, cols] += _pick(dvs[0], dvs[1], lanes_k)
            dk_sc[:, cols] += _pick(dks[0], dks[1], lanes_k)
            return carry

        for p in range(pairs):
            pair(p, 0)

    @pl.when(i == pl.num_programs(1) - 1)
    def _():
        dk_ref[...] = dk_sc[...]
        dv_ref[...] = dv_sc[...]


def _attn_bwd(lo_ref, hi_ref, q_ref, k_ref, v_ref, qs_ref, ks_ref, lse_ref, dl_ref, do_ref, dk_ref, dv_ref, dq_ref, dk_sc, dv_sc):
    j = pl.program_id(0)
    i = pl.program_id(1)
    qb = lo_ref[j] + i
    pairs = q_ref.shape[1] // LANES
    bq = q_ref.shape[0]
    bk = k_ref.shape[0]

    @pl.when((j == 0) & (i == 0))
    def _():
        dq_ref[...] = jnp.zeros_like(dq_ref)

    @pl.when(i == 0)
    def _():
        dk_sc[...] = jnp.zeros_like(dk_sc)
        dv_sc[...] = jnp.zeros_like(dv_sc)

    @pl.when(qb <= hi_ref[j])
    def _():
        mask = qs_ref[...] == ks_ref[...]
        lanes_q = _lanes(bq)
        lanes_k = _lanes(bk)
        rows = pl.ds(pl.multiple_of(qb * bq, bq), bq)
        for p in range(pairs):
            cols = pl.ds(p * LANES, LANES)
            q2 = q_ref[:, cols]
            k2 = k_ref[:, cols]
            v2 = v_ref[:, cols]
            do2 = do_ref[:, cols]
            zero = jnp.zeros_like(q2)
            dks, dvs, dqs = [], [], []
            for h in range(2):
                sel = (lambda a: _pick(a, zero, lanes_q)) if h == 0 else (lambda a: _pick(zero, a, lanes_q))
                s = _nt(sel(q2), k2)
                e = jnp.where(mask, jnp.exp(s - lse_ref[2 * p + h]), 0.0)
                dp = _nt(sel(do2), v2)
                ds = (e * (dp - dl_ref[2 * p + h])).astype(jnp.bfloat16)
                dvs.append(_tn(e.astype(jnp.bfloat16), do2))
                dks.append(_tn(ds, q2))
                dqs.append(_nn(ds, k2))
            dv_sc[:, cols] += _pick(dvs[0], dvs[1], lanes_k)
            dk_sc[:, cols] += _pick(dks[0], dks[1], lanes_k)
            dq_ref[rows, cols] += _pick(dqs[0], dqs[1], lanes_q)

    @pl.when(i == pl.num_programs(1) - 1)
    def _():
        dk_ref[...] = dk_sc[...]
        dv_ref[...] = dv_sc[...]

    @pl.when((i == pl.num_programs(1) - 1) & (j == pl.num_programs(0) - 1))
    def _():
        dq_ref[...] = dq_ref[...] * 0.125


def _clamp(start, step, last):
    return jnp.minimum(start + step, jnp.maximum(last, 0))


def _params():
    return pltpu.CompilerParams(dimension_semantics=("arbitrary", "arbitrary"), vmem_limit_bytes=48 * 1024 * 1024)


def flash_forward(q, k, v, q_ids, k_ids, lo, hi, block_q, block_k, steps):
    nq, width = q.shape
    nk = k.shape[0]
    heads = width // 64
    kv_map = lambda i, j, a, b: (_clamp(a[i], j, b[i]), 0)
    ks_map = lambda i, j, a, b: (0, _clamp(a[i], j, b[i]))
    row = lambda i, j, a, b: (i, 0)
    grid_spec = pltpu.PrefetchScalarGridSpec(
        num_scalar_prefetch=2,
        grid=(nq // block_q, steps),
        in_specs=[
            pl.BlockSpec((block_q, width), row),
            pl.BlockSpec((block_k, width), kv_map),
            pl.BlockSpec((block_k, width), kv_map),
            pl.BlockSpec((block_q, 1), row),
            pl.BlockSpec((1, block_k), ks_map),
        ],
        out_specs=[
            pl.BlockSpec((block_q, width), row),
            pl.BlockSpec((heads, block_q, 1), lambda i, j, a, b: (0, i, 0)),
        ],
        scratch_shapes=[
            pltpu.VMEM((heads, block_q, 1), jnp.float32),
            pltpu.VMEM((heads, block_q, 1), jnp.float32),
            pltpu.VMEM((block_q, width), jnp.float32),
        ],
    )
    return pl.pallas_call(
        _attn_fwd,
        grid_spec=grid_spec,
        cost_estimate=pl.CostEstimate(flops=8 * nq * LONGEST * width, transcendentals=nq * LONGEST * heads, bytes_accessed=2 * (nq + 2 * nk) * width * 2),
        out_shape=[jax.ShapeDtypeStruct((nq, width), jnp.float32), jax.ShapeDtypeStruct((heads, nq, 1), jnp.float32)],
        compiler_params=_params(),
    )(lo, hi, q, k, v, q_ids.reshape(nq, 1), k_ids.reshape(1, nk))


def flash_dq(q, k, v, q_ids, k_ids, lse, delta, do, lo, hi, block_q, block_k, steps):
    nq, width = q.shape
    nk = k.shape[0]
    heads = width // 64
    kv_map = lambda i, j, a, b: (_clamp(a[i], j, b[i]), 0)
    ks_map = lambda i, j, a, b: (0, _clamp(a[i], j, b[i]))
    row = lambda i, j, a, b: (i, 0)
    hrow = lambda i, j, a, b: (0, i, 0)
    grid_spec = pltpu.PrefetchScalarGridSpec(
        num_scalar_prefetch=2,
        grid=(nq // block_q, steps),
        in_specs=[
            pl.BlockSpec((block_q, width), row),
            pl.BlockSpec((block_k, width), kv_map),
            pl.BlockSpec((block_k, width), kv_map),
            pl.BlockSpec((block_q, 1), row),
            pl.BlockSpec((1, block_k), ks_map),
            pl.BlockSpec((heads, block_q, 1), hrow),
            pl.BlockSpec((heads, block_q, 1), hrow),
            pl.BlockSpec((block_q, width), row),
        ],
        out_specs=pl.BlockSpec((block_q, width), row),
        scratch_shapes=[pltpu.VMEM((block_q, width), jnp.float32)],
    )
    return pl.pallas_call(
        _attn_dq,
        grid_spec=grid_spec,
        out_shape=jax.ShapeDtypeStruct((nq, width), jnp.float32),
        compiler_params=_params(),
    )(lo, hi, q, k, v, q_ids.reshape(nq, 1), k_ids.reshape(1, nk), lse, delta, do)


def flash_dkv(q, k, v, q_ids, k_ids, lse, delta, do, qlo, qhi, block_q, block_k, steps):
    nq, width = q.shape
    nk = k.shape[0]
    heads = width // 64
    q_map = lambda j, i, a, b: (_clamp(a[j], i, b[j]), 0)
    h_map = lambda j, i, a, b: (0, _clamp(a[j], i, b[j]), 0)
    col = lambda j, i, a, b: (j, 0)
    grid_spec = pltpu.PrefetchScalarGridSpec(
        num_scalar_prefetch=2,
        grid=(nk // block_k, steps),
        in_specs=[
            pl.BlockSpec((block_q, width), q_map),
            pl.BlockSpec((block_k, width), col),
            pl.BlockSpec((block_k, width), col),
            pl.BlockSpec((block_q, 1), q_map),
            pl.BlockSpec((1, block_k), lambda j, i, a, b: (0, j)),
            pl.BlockSpec((heads, block_q, 1), h_map),
            pl.BlockSpec((heads, block_q, 1), h_map),
            pl.BlockSpec((block_q, width), q_map),
        ],
        out_specs=[pl.BlockSpec((block_k, width), col), pl.BlockSpec((block_k, width), col)],
        scratch_shapes=[pltpu.VMEM((block_k, width), jnp.float32), pltpu.VMEM((block_k, width), jnp.float32)],
    )
    return pl.pallas_call(
        _attn_dkv,
        grid_spec=grid_spec,
        out_shape=[jax.ShapeDtypeStruct((nk, width), jnp.float32), jax.ShapeDtypeStruct((nk, width), jnp.float32)],
        compiler_params=_params(),
    )(qlo, qhi, q, k, v, q_ids.reshape(nq, 1), k_ids.reshape(1, nk), lse, delta, do)


def flash_backward(q, k, v, q_ids, k_ids, lse, delta, do, qlo, qhi, block_q, block_k, steps):
    nq, width = q.shape
    nk = k.shape[0]
    heads = width // 64
    q_map = lambda j, i, a, b: (_clamp(a[j], i, b[j]), 0)
    h_map = lambda j, i, a, b: (0, _clamp(a[j], i, b[j]), 0)
    col = lambda j, i, a, b: (j, 0)
    grid_spec = pltpu.PrefetchScalarGridSpec(
        num_scalar_prefetch=2,
        grid=(nk // block_k, steps),
        in_specs=[
            pl.BlockSpec((block_q, width), q_map),
            pl.BlockSpec((block_k, width), col),
            pl.BlockSpec((block_k, width), col),
            pl.BlockSpec((block_q, 1), q_map),
            pl.BlockSpec((1, block_k), lambda j, i, a, b: (0, j)),
            pl.BlockSpec((heads, block_q, 1), h_map),
            pl.BlockSpec((heads, block_q, 1), h_map),
            pl.BlockSpec((block_q, width), q_map),
        ],
        out_specs=[
            pl.BlockSpec((block_k, width), col),
            pl.BlockSpec((block_k, width), col),
            pl.BlockSpec((nq, width), lambda j, i, a, b: (0, 0)),
        ],
        scratch_shapes=[pltpu.VMEM((block_k, width), jnp.float32), pltpu.VMEM((block_k, width), jnp.float32)],
    )
    return pl.pallas_call(
        _attn_bwd,
        grid_spec=grid_spec,
        cost_estimate=pl.CostEstimate(flops=20 * nq * LONGEST * width, transcendentals=nq * LONGEST * heads, bytes_accessed=4 * (2 * nq + 4 * nk) * width),
        out_shape=[
            jax.ShapeDtypeStruct((nk, width), jnp.float32),
            jax.ShapeDtypeStruct((nk, width), jnp.float32),
            jax.ShapeDtypeStruct((nq, width), jnp.float32),
        ],
        compiler_params=_params(),
    )(qlo, qhi, q, k, v, q_ids.reshape(nq, 1), k_ids.reshape(1, nk), lse, delta, do)


def block_ranges(q_ids, k_ids, q_start, q_end, block_q, block_k):
    nq = q_ids.shape[0]
    nk = k_ids.shape[0]
    nqb, nkb = nq // block_q, nk // block_k
    first = q_start.reshape(nqb, block_q)[:, 0]
    last = q_end.reshape(nqb, block_q)[:, block_q - 1]
    lo = jnp.clip(first // block_k, 0, nkb - 1).astype(jnp.int32)
    hi = jnp.clip((last - 1) // block_k, 0, nkb - 1).astype(jnp.int32)
    kb = jnp.arange(nkb, dtype=jnp.int32)
    qb = jnp.arange(nqb, dtype=jnp.int32)
    cover = (lo[:, None] <= kb[None, :]) & (kb[None, :] <= hi[:, None])
    qlo = jnp.min(jnp.where(cover, qb[:, None], nqb), axis=0).astype(jnp.int32)
    qhi = jnp.max(jnp.where(cover, qb[:, None], -1), axis=0).astype(jnp.int32)
    return lo, hi, qlo, qhi


def norm_forward(values, gain, shift):
    center = jnp.mean(values, axis=-1, keepdims=True)
    offsets = values - center
    spread = jnp.mean(offsets * offsets, axis=-1, keepdims=True)
    inverse = lax.rsqrt(spread + 1e-06)
    normed = offsets * inverse
    return (normed * gain + shift, normed, inverse)


def norm_backward(grad_y, normed, inverse, gain):
    grad_normed = grad_y * gain
    mean_one = jnp.mean(grad_normed, axis=-1, keepdims=True)
    mean_two = jnp.mean(grad_normed * normed, axis=-1, keepdims=True)
    return inverse * (grad_normed - mean_one - normed * mean_two)


def activate(values):
    return jax.nn.gelu(values, approximate=False)


def contract_last(left, right):
    return lax.dot_general(left, right, (((1,), (1,)), ((), ())), preferred_element_type=jnp.float32)


def contract_first(left, right):
    return lax.dot_general(left, right, (((0,), (0,)), ((), ())), preferred_element_type=jnp.float32)


def column_sum(values):
    return jnp.sum(values.astype(jnp.float32), axis=0)


def group_segments(lengths, dealing, group_index, group_rows, per_group):
    picked = lax.dynamic_slice_in_dim(dealing, group_index * per_group, per_group)
    match = picked[:, None] == jnp.arange(lengths.shape[0], dtype=jnp.int32)[None, :]
    chosen = jnp.sum(jnp.where(match, lengths[None, :], 0), axis=1)
    ends = jnp.cumsum(chosen)
    starts = ends - chosen
    places = jnp.arange(group_rows, dtype=jnp.int32)
    segment_ids = jnp.sum((places[:, None] >= ends[None, :]).astype(jnp.int32), axis=1)
    return (segment_ids, starts, ends)


def cyclic_pieces(piece):
    count = lax.axis_size("tensor")
    me = lax.axis_index("tensor")
    got = [piece]
    for k in range(1, count):
        got.append(lax.ppermute(piece, "tensor", [(s, (s + k) % count) for s in range(count)]))
    order = (me - jnp.arange(count, dtype=jnp.int32)) % count
    return jnp.take(jnp.stack(got), order, axis=0)


def gather_weights(blocks):
    count = lax.axis_size("tensor")
    widths = [b.shape[1] for b in blocks]
    piece = jnp.concatenate(blocks, axis=1)
    parts = cyclic_pieces(piece)
    cols, at = [], 0
    for w in widths:
        cols.extend(parts[t, :, at:at + w] for t in range(count))
        at += w
    strip = jnp.concatenate(cols, axis=1)
    full = lax.all_gather(strip, "dp", axis=0, tiled=True)
    out, at = [], 0
    for w in widths:
        out.append(full[:, at:at + w * count])
        at += w * count
    return out


def vector_rows(v, rows):
    dp = lax.axis_size("dp")
    slab = rows // dp
    spread = v.reshape(dp, 1, -1)
    return jnp.pad(spread, ((0, 0), (0, slab - 1), (0, 0))).reshape(rows, -1)


def pack_grads(grads, vectors):
    count = lax.axis_size("tensor")
    me = lax.axis_index("tensor")
    rows = grads[0].shape[0]
    mats = [g.astype(jnp.bfloat16) for g in grads] + [vector_rows(v.astype(jnp.bfloat16), rows) for v in vectors]
    widths = [m.shape[1] // count for m in mats]
    cat = jnp.concatenate(mats, axis=1)
    return widths, cat


def reduce_dp(cat):
    return lax.psum_scatter(cat, "dp", scatter_dimension=0, tiled=True)


def reduce_dp_by_halves(cat):
    dp = lax.axis_size("dp")
    me = lax.axis_index("dp")
    slab = cat.shape[0] // dp
    part = cat.astype(jnp.float32).reshape(dp, slab, cat.shape[1])
    bit = 0
    while (1 << bit) < dp:
        mine = (me >> bit) % 2
        halves = part.reshape(part.shape[0] // 2, 2, slab, cat.shape[1])
        keep = lax.dynamic_index_in_dim(halves, mine, axis=1, keepdims=False)
        send = lax.dynamic_index_in_dim(halves, 1 - mine, axis=1, keepdims=False)
        pairs = [(i, i ^ (1 << bit)) for i in range(dp)]
        part = keep + lax.ppermute(send.astype(jnp.bfloat16), "dp", pairs).astype(jnp.float32)
        bit += 1
    return part.reshape(slab, cat.shape[1])


def reduce_tensor(strip, widths, n_grads):
    count = lax.axis_size("tensor")
    me = lax.axis_index("tensor")
    strip = strip.astype(jnp.float32)
    per_t = []
    for t in range(count):
        at, cols = 0, []
        for w in widths:
            cols.append(strip[:, at + t * w:at + (t + 1) * w])
            at += w * count
        per_t.append(jnp.concatenate(cols, axis=1))
    stacked = jnp.stack(per_t)
    total = jnp.take(stacked, me, axis=0)
    for k in range(1, count):
        send = jnp.take(stacked, (me + k) % count, axis=0)
        total = total + lax.ppermute(send, "tensor", [(s, (s + k) % count) for s in range(count)])
    out, at = [], 0
    for i, w in enumerate(widths):
        block = total[:, at:at + w]
        at += w
        out.append(block if i < n_grads else block[0])
    return out


def halo_plan(rows):
    hops = -(-LONGEST // rows)
    takes = [rows] * (hops - 1) + [LONGEST - rows * (hops - 1)]
    return takes


def shift_rows(values, distance, count):
    if distance >= count:
        return jnp.zeros_like(values)
    if distance > 0:
        pairs = [(s, s + distance) for s in range(count - distance)]
    else:
        pairs = [(s - distance, s) for s in range(count + distance)]
    return lax.ppermute(values, "tensor", pairs)


def build_window(own, takes, count):
    rows = own.shape[0]
    left = [shift_rows(own[rows - take:], d + 1, count) for d, take in enumerate(takes)]
    right = [shift_rows(own[:take], -(d + 1), count) for d, take in enumerate(takes)]
    return jnp.concatenate(left[::-1] + [own] + right, axis=0)


def return_window(values, takes, count):
    rows = values.shape[0] - 2 * LONGEST
    total = values[LONGEST:LONGEST + rows]
    at = LONGEST
    for d, take in enumerate(takes):
        piece = values[at - take:at].astype(jnp.bfloat16)
        at -= take
        back = shift_rows(piece, -(d + 1), count).astype(jnp.float32)
        total = total + jnp.pad(back, ((rows - take, 0), (0, 0)))
    at = LONGEST + rows
    for d, take in enumerate(takes):
        piece = values[at:at + take].astype(jnp.bfloat16)
        at += take
        back = shift_rows(piece, d + 1, count).astype(jnp.float32)
        total = total + jnp.pad(back, ((0, rows - take), (0, 0)))
    return total


def to_heads(values):
    rows, width = values.shape
    return values.reshape(rows, width // HEAD_DIM, HEAD_DIM).transpose(1, 0, 2)


def from_heads(values):
    heads, rows, hd = values.shape
    return values.transpose(1, 0, 2).reshape(rows, heads * hd)


def shards(tokens, lengths, dealing, w_query, w_key, w_value, w_out, w_inner, w_outer, b_query, b_value, b_out, b_inner, b_outer, gain_attn, shift_attn, gain_ffn, shift_ffn, grad_out):
    count = lax.axis_size("tensor")
    tens_index = lax.axis_index("tensor")
    group_index = lax.axis_index("dp")
    rows = tokens.shape[0]
    group_rows = rows * count
    per_group = lengths.shape[0] // lax.axis_size("dp")
    takes = halo_plan(rows)
    window = rows + 2 * LONGEST
    seg, starts, ends = group_segments(lengths, dealing, group_index, group_rows, per_group)
    base = rows * tens_index - LONGEST
    places = base + jnp.arange(window, dtype=jnp.int32)
    valid = (places >= 0) & (places < group_rows)
    k_ids = jnp.where(valid, jnp.sum((places[:, None] >= ends[None, :]).astype(jnp.int32), axis=1), -1).astype(jnp.int32)
    q_ids = lax.dynamic_slice_in_dim(seg, rows * tens_index, rows)
    q_start = jnp.take(starts, q_ids) - base
    q_end = jnp.take(ends, q_ids) - base
    lo, hi, qlo, qhi = block_ranges(q_ids, k_ids, q_start, q_end, BLOCK, BLOCK)
    nkb = window // BLOCK
    kv_steps = min(nkb, (BLOCK + 2 * (LONGEST - 1)) // BLOCK + 2)
    q_steps = rows // BLOCK

    wq, wk, wv = gather_weights([w_query, w_key, w_value])
    wo_t, wi, wf_t = gather_weights([w_out.T, w_inner, w_outer.T])
    gain_one = gain_attn.astype(jnp.float32)
    gain_two = gain_ffn.astype(jnp.float32)

    x_own = tokens
    x_win = build_window(tokens, takes, count)
    query = (jnp.dot(x_own, wq, preferred_element_type=jnp.float32) + b_query.astype(jnp.float32)).astype(jnp.bfloat16)
    key_w = jnp.dot(x_win, wk, preferred_element_type=jnp.float32).astype(jnp.bfloat16)
    value_w = (jnp.dot(x_win, wv, preferred_element_type=jnp.float32) + b_value.astype(jnp.float32)).astype(jnp.bfloat16)
    scaled = query * jnp.asarray(1.0 / math.sqrt(HEAD_DIM), jnp.bfloat16)
    ctx32, lse = flash_forward(scaled, key_w, value_w, q_ids, k_ids, lo, hi, BLOCK, BLOCK, kv_steps)
    context = ctx32.astype(jnp.bfloat16)
    attn = contract_last(context, wo_t) + b_out.astype(jnp.float32)
    hidden, norm_one, inverse_one = norm_forward(tokens.astype(jnp.float32) + attn, gain_one, shift_attn.astype(jnp.float32))
    hidden_low = hidden.astype(jnp.bfloat16)
    pre_act = jnp.dot(hidden_low, wi, preferred_element_type=jnp.float32) + b_inner.astype(jnp.float32)
    act = activate(pre_act).astype(jnp.bfloat16)
    ffn = contract_last(act, wf_t) + b_outer.astype(jnp.float32)
    output, norm_two, inverse_two = norm_forward(hidden + ffn, gain_two, shift_ffn.astype(jnp.float32))

    grad_y = grad_out.astype(jnp.float32)
    grad_resid_two = norm_backward(grad_y, norm_two, inverse_two, gain_two)
    grad_ffn = grad_resid_two.astype(jnp.bfloat16)
    grad_outer_t = contract_first(grad_ffn, act)
    grad_act = jnp.dot(grad_ffn, wf_t, preferred_element_type=jnp.float32)
    unused, gelu_pull = jax.vjp(activate, pre_act)
    grad_pre = gelu_pull(grad_act)[0].astype(jnp.bfloat16)
    grad_inner_w = contract_first(hidden_low, grad_pre)
    grad_hidden = grad_resid_two + contract_last(grad_pre, wi)
    grad_resid_one = norm_backward(grad_hidden, norm_one, inverse_one, gain_one)
    grad_attn = grad_resid_one.astype(jnp.bfloat16)
    grad_out_t = contract_first(grad_attn, context)
    grad_context = jnp.dot(grad_attn, wo_t, preferred_element_type=jnp.float32).astype(jnp.bfloat16)
    late = [
        column_sum(grad_attn),
        column_sum(grad_pre),
        column_sum(grad_ffn),
        jnp.sum(grad_hidden * norm_one, axis=0),
        jnp.sum(grad_hidden, axis=0),
        jnp.sum(grad_y * norm_two, axis=0),
        jnp.sum(grad_y, axis=0),
    ]
    early_widths, early_cat = pack_grads([grad_out_t, grad_inner_w, grad_outer_t], late)
    grad_context, early_cat = lax.optimization_barrier((grad_context, early_cat))
    early_strip = reduce_dp(early_cat)
    heads = query.shape[1] // HEAD_DIM
    delta = jnp.sum((grad_context.astype(jnp.float32) * ctx32).reshape(rows, heads, HEAD_DIM), axis=-1)
    delta = delta.T.reshape(heads, rows, 1)
    dk_h, dv_h, dq_h = flash_backward(scaled, key_w, value_w, q_ids, k_ids, lse, delta, grad_context, qlo, qhi, BLOCK, BLOCK, q_steps)
    early_strip, dq_h, dk_h, dv_h = lax.optimization_barrier((early_strip, dq_h, dk_h, dv_h))
    early_sums = reduce_tensor(early_strip, early_widths, 3)
    g_out_t, g_inner, g_outer_t = early_sums[:3]
    late = early_sums[3:]
    grad_query = dq_h.astype(jnp.bfloat16)
    grad_key = dk_h.astype(jnp.bfloat16)
    grad_value = dv_h.astype(jnp.bfloat16)
    grad_query_w = contract_first(x_own, grad_query)
    grad_key_w = contract_first(x_win, grad_key)
    grad_value_w = contract_first(x_win, grad_value)
    grad_win = contract_last(grad_key, wk) + contract_last(grad_value, wv)
    grad_tokens = grad_resid_one + contract_last(grad_query, wq) + return_window(grad_win, takes, count)

    late_widths, late_cat = pack_grads(
        [grad_query_w, grad_key_w, grad_value_w], [column_sum(grad_query), column_sum(grad_value)]
    )
    g_query, g_key, g_value, g_bq, g_bv = reduce_tensor(reduce_dp_by_halves(late_cat), late_widths, 3)
    summed = (g_query, g_key, g_value, g_out_t.T, g_inner, g_outer_t.T)
    small = [g_bq, g_bv] + late
    return (output.astype(jnp.bfloat16), grad_tokens) + summed + tuple(small)


def solution(mesh):
    rows = P(("dp", "tensor"), None)
    vec = P(("dp", "tensor"))
    return jax.shard_map(
        shards,
        mesh=mesh,
        in_specs=(rows, P(), P(), P("dp", "tensor"), P("dp", "tensor"), P("dp", "tensor"), P("tensor", "dp"), P("dp", "tensor"), P("tensor", "dp"), P(), P(), P(), P(), P(), P(), P(), P(), P(), rows),
        out_specs=(rows, rows, P("dp", "tensor"), P("dp", "tensor"), P("dp", "tensor"), P("tensor", "dp"), P("dp", "tensor"), P("tensor", "dp")) + (vec,) * 9,
        check_vma=False,
    )
```

profile of v0, /device:TPU:9, one launch (start us, length us, event | category | flops | bytes accessed | tf_op | source)
XLA Modules:
  0.0 621.5 jit_solution(4159249557530035844)
XLA Ops:
  13.0 6.4 %collective-permute-done.1 = bf16[96,576]{1,0:T(8,128)(2,1)S(1)} collective-permute-done((bf16[96,576]{1,0:T(8,128)(2,1)S(1)}, bf16[96,576]{1,0:T(8,128)(2,1)S(1)}, u32[]{:S(2)}, u32[]{:S(2)}) %collective-permute-start.1) | collective-permute-done | bytes 110624 | tf_op jit(solution)/shard_map/ppermute | solution.py:451
  26.6 7.3 %collective-permute-done.7 = bf16[96,1728]{1,0:T(8,128)(2,1)S(1)} collective-permute-done((bf16[96,1728]{1,0:T(8,128)(2,1)S(1)}, bf16[96,1728]{1,0:T(8,128)(2,1)S(1)}, u32[]{:S(2)}, u32[]{:S(2)}) %collective-permute-start.7) | collective-permute-done | bytes 331808 | tf_op jit(solution)/shard_map/ppermute | solution.py:451
  33.9 20.2 %collective-permute-done.8 = bf16[96,1728]{1,0:T(8,128)(2,1)S(1)} collective-permute-done((bf16[96,1728]{1,0:T(8,128)(2,1)S(1)}, bf16[96,1728]{1,0:T(8,128)(2,1)S(1)}, u32[]{:S(2)}, u32[]{:S(2)}) %collective-permute-start.8) | collective-permute-done | bytes 331808 | tf_op jit(solution)/shard_map/ppermute | solution.py:451
  61.9 4.4 collective-permute-start.5
  67.2 3.7 collective-permute-start.3
  74.2 3.3 select_subtract_fusion
  85.9 18.1 %collective-permute-done.3 = bf16[256,768]{1,0:T(8,128)(2,1)} collective-permute-done((bf16[256,768]{1,0:T(8,128)(2,1)}, bf16[256,768]{1,0:T(8,128)(2,1)}, u32[]{:S(2)}, u32[]{:S(2)}) %collective-permute-start.3) | collective-permute-done | bytes 393248 | tf_op jit(solution)/shard_map/ppermute | solution.py:549
  115.0 8.3 %convolution_convert_fusion.2.k_ref = bf16[2816,768]{1,0:T(8,128)(2,1)} fusion(bf16[2816,768]{1,0:T(8,128)(2,1)} %constant_dynamic-update-slice_fusion, bf16[768,2304]{1,0:T(8,128)(2,1)S(1)} %copy-done.18), kind=kOutput, calls=%fused_computation.23 | convolution fusion | flops 3324051456 | bytes 9830400 | tf_op jit(solution)/shard_map/dot_general | solution.py:617
  123.3 7.9 %add_convert_fusion.1.v_ref = bf16[2816,768]{1,0:T(8,128)(2,1)} fusion(bf16[2816,768]{1,0:T(8,128)(2,1)} %constant_dynamic-update-slice_fusion, f32[768]{0:T(1024)S(1)} %convert_element_type.221, bf16[768,2304]{1,0:T(8,128)(2,1)S(1)} %copy-done.18), kind=kOutput, calls=%fused_computation.19 | convolution fusion | flops 3326214144 | bytes 9834496 | tf_op jit(solution)/shard_map/dot_general | solution.py:618
  131.2 85.7 %shard_map.314 = (f32[768,768]{1,0:T(8,128)S(1)}, f32[12,768,1]{2,1,0:T(8,128)}) custom-call(s32[3]{0:T(128)S(1)} %fusion.76.lo_ref, s32[3]{0:T(128)S(1)} %fusion.75.hi_ref, bf16[768,768]{1,0:T(8,128)(2,1)S(1)} %fusion.42.q_ref, bf16[2816,768]{1,0:T(8,128)(2,1)} %convolution_convert_fusion.2.k_ref, bf16[2816,768]{1,0:T(8,128)(2,1)} %add_convert_fusion.1.v_ref, ...), custom_call_target="tpu_custom_call" | custom-call | flops 4831838208 | bytes 19660800 | tf_op jit(solution)/shard_map/pallas_call | solution.py:275
  220.0 29.6 %multiply_convert_fusion = (bf16[768,3072]{1,0:T(8,128)(2,1)S(1)}, f32[768,3072]{1,0:T(8,128)}, f32[768,3072]{1,0:T(8,128)}) fusion(f32[3072]{0:T(1024)S(1)} %convert_element_type.229, bf16[768,6912]{1,0:T(8,128)(2,1)} %all-gather.5.cloned.1.call-done, f32[768,768]{0,1:T(8,128)S(1)} %get-tuple-element.279, f32[768]{0:T(1024)S(1)} %convert_element_type.227, ...), kind=kOutput, calls=%fused_computation.5 | convolution fusion | flops 3782541312 | bytes 30695424 | tf_op jit(solution)/shard_map/dot_general | solution.py:625
  249.6 6.0 fusion.102
  261.2 5.5 convolution_convert_fusion
  266.7 13.7 %fusion.103 = (bf16[3072]{0:T(1024)(128)(2,1)}, bf16[768,3072]{1,0:T(8,128)(2,1)S(1)}) fusion(f32[768,3072]{1,0:T(8,128)} %get-tuple-element.150, bf16[768,768]{0,1:T(8,128)(2,1)S(1)} %get-tuple-element.146, bf16[768,6912]{1,0:T(8,128)(2,1)} %all-gather.5.cloned.1.call-done, f32[768,3072]{1,0:T(8,128)} %get-tuple-element.280, ...), kind=kOutput, calls=%fused_computation.250 | convolution fusion | flops 3661624320 | bytes 29509632 | tf_op jit(solution)/shard_map/dot_general | solution.py:634
  280.4 5.9 convolution_convert_fusion.1
  286.3 7.9 %multiply_reduce_fusion = (bf16[768]{0:T(1024)(128)(2,1)}, f32[768]{0:T(1024)S(1)}, f32[768]{0:T(1024)S(1)}, bf16[768]{0:T(1024)(128)(2,1)}, f32[768,768]{0,1:T(8,128)S(1)}) fusion(f32[768,768]{0,1:T(8,128)S(1)} %get-tuple-element.279, f32[768]{0:T(1024)S(1)} %add_rsqrt_fusion.1, f32[768]{0:T(1024)S(1)} %broadcast_multiply_fusion.5, ...), kind=kOutput, calls=%fused_computation.50 | convolution fusion | flops 3634492416 | bytes 17728512 | tf_op jit(solution)/shard_map/dot_general | solution.py:424
  311.1 18.3 %concatenate.61 = bf16[768,7872]{1,0:T(8,128)(2,1)} concatenate(bf16[768,768]{1,0:T(8,128)(2,1)S(1)} %copy.121, bf16[768,3072]{1,0:T(8,128)(2,1)} %convolution_convert_fusion.1, bf16[768,3072]{1,0:T(8,128)(2,1)} %convolution_convert_fusion, bf16[768,96]{1,0:T(8,128)(2,1)} %bitcast.190, bf16[768,384]{1,0:T(8,128)(2,1)} %bitcast.182, bf16[768,96]{1,0:T(8,128)(2,1)} %bitcast.193, ...), dimensions={1} | concatenate | bytes 24182784 | tf_op jit(solution)/shard_map/concatenate | solution.py:487
  338.8 4.5 copy.124.dl_ref
  347.9 97.4 %shard_map.315 = (f32[2816,768]{1,0:T(8,128)}, f32[2816,768]{1,0:T(8,128)}, f32[768,768]{1,0:T(8,128)S(1)}) custom-call(s32[11]{0:T(128)S(1)} %copy-done.2, s32[11]{0:T(128)S(1)} %get-tuple-element.143.hi_ref, bf16[768,768]{1,0:T(8,128)(2,1)S(1)} %copy-done.4, bf16[2816,768]{1,0:T(8,128)(2,1)} %convolution_convert_fusion.2.k_ref, ...), custom_call_target="tpu_custom_call" | custom-call | flops 12079595520 | bytes 39321600 | tf_op jit(solution)/shard_map/pallas_call | solution.py:374
  455.7 5.9 convolution_convert_fusion.3
  477.5 8.4 %fusion.38 = bf16[768,768]{1,0:T(8,128)(2,1)S(1)} fusion(bf16[2816,768]{1,0:T(8,128)(2,1)} %constant_dynamic-update-slice_fusion, f32[2816,768]{1,0:T(8,128)} %get-tuple-element.39), kind=kOutput, calls=%fused_computation.72 | convolution fusion | flops 3324641280 | bytes 14155776 | tf_op jit(solution)/shard_map/dot_general | solution.py:428
  490.9 6.7 %concatenate.67 = bf16[4,2,96,2496]{3,2,0,1:T(8,128)(2,1)} concatenate(bf16[4,2,96,768]{3,2,0,1:T(8,128)(2,1)} %copy.128, bf16[4,2,96,768]{3,2,0,1:T(8,128)(2,1)S(1)} %copy-done.17, bf16[4,2,96,768]{3,2,0,1:T(8,128)(2,1)} %copy.130, bf16[4,2,96,96]{3,2,0,1:T(8,128)(2,1)} %copy.131, bf16[4,2,96,96]{3,2,0,1:T(8,128)(2,1)} %copy.132), dimensions={3} | concatenate | bytes 7667712 | tf_op jit(solution)/shard_map/concatenate | solution.py:487
  505.4 5.6 collective-permute-start.14
  510.9 10.6 %fusion.29 = f32[2816,768]{0,1:T(8,128)} fusion(f32[2816,768]{1,0:T(8,128)} %get-tuple-element.39, bf16[768,2304]{1,0:T(8,128)(2,1)} %all-gather.3.cloned.1.call-done), kind=kOutput, calls=%fused_computation.64 | convolution fusion | flops 3324051456 | bytes 18481152 | tf_op jit(solution)/shard_map/dot_general | solution.py:424
  521.5 8.8 %fusion.104 = (bf16[2816,768]{0,1:T(8,128)(2,1)S(1)}, f32[2816,768]{0,1:T(8,128)}) fusion(f32[2816,768]{0,1:T(8,128)} %fusion.29, bf16[768,2304]{1,0:T(8,128)(2,1)} %all-gather.3.cloned.1.call-done, f32[2816,768]{1,0:T(8,128)S(1)} %bitcast.172), kind=kOutput, calls=%fused_computation.251 | convolution fusion | flops 3328376832 | bytes 31457280 | tf_op jit(solution)/shard_map/dot_general | solution.py:424
  532.0 4.0 collective-permute-start.10
  543.6 6.4 %collective-permute-start.13 = (bf16[256,768]{0,1:T(8,128)(2,1)}, bf16[256,768]{0,1:T(8,128)(2,1)}, u32[]{:S(2)}, u32[]{:S(2)}) collective-permute-start(bf16[256,768]{0,1:T(8,128)(2,1)} %get-tuple-element.159), channel_id=1, source_target_pairs={{0,2},{1,3},{4,6},{5,7},{8,10},{9,11},{12,14},{13,15},{16,18},{17,... | collective-permute-start | bytes 1179656 | tf_op jit(solution)/shard_map/ppermute | solution.py:549
  552.1 10.0 %collective-permute-done.15 = bf16[2,96,2496]{2,1,0:T(8,128)(2,1)S(1)} collective-permute-done((bf16[2,96,2496]{2,1,0:T(8,128)(2,1)S(1)}, bf16[2,96,2496]{2,1,0:T(8,128)(2,1)S(1)}, u32[]{:S(2)}, u32[]{:S(2)}) %collective-permute-start.15) | collective-permute-done | bytes 958496 | tf_op jit(solution)/shard_map/ppermute | solution.py:507
  567.4 8.6 %collective-permute-done.16 = bf16[1,96,2496]{2,1,0:T(8,128)(2,1)} collective-permute-done((bf16[1,96,2496]{2,1,0:T(8,128)(2,1)}, bf16[1,96,2496]{2,1,0:T(8,128)(2,1)}, u32[]{:S(2)}, u32[]{:S(2)}) %collective-permute-start.16) | collective-permute-done | bytes 479264 | tf_op jit(solution)/shard_map/ppermute | solution.py:507
  590.4 5.6 fusion.26
  599.0 7.9 %collective-permute-done.18 = f32[96,624]{1,0:T(8,128)} collective-permute-done((f32[96,624]{1,0:T(8,128)}, f32[96,624]{1,0:T(8,128)}, u32[]{:S(2)}, u32[]{:S(2)}) %collective-permute-start.18) | collective-permute-done | bytes 239648 | tf_op jit(solution)/shard_map/ppermute | solution.py:527
  606.9 5.3 collective-permute-done.19
  (257 shorter events, 158.8 us)
Async XLA Ops:
  7.2 105.3 %all-gather.3.cloned.1.call-start = ((), (), s32[]{:S(2)}) async-start(), calls=%async_computation.1 | async-start | bytes 3981312 | tf_op jit(solution)/shard_map/all_gather | solution.py:466
  8.2 4.8 collective-permute-start
  9.5 9.9 %collective-permute-start.1 = (bf16[96,576]{1,0:T(8,128)(2,1)S(1)}, bf16[96,576]{1,0:T(8,128)(2,1)S(1)}, u32[]{:S(2)}, u32[]{:S(2)}) collective-permute-start(bf16[96,576]{1,0:T(8,128)(2,1)S(1)} %pad_maximum_fusion.4), channel_id=1, source_target_pairs={{0,2},{1,3},{2,0},{3,1},{4,6},{5,7},{6,4},{7,5},{8,10},{9,11},{10,... | collective-permute-start | bytes 331784 | tf_op jit(solution)/shard_map/ppermute | solution.py:451
  10.6 11.6 %collective-permute-start.2 = (bf16[96,576]{1,0:T(8,128)(2,1)S(1)}, bf16[96,576]{1,0:T(8,128)(2,1)S(1)}, u32[]{:S(2)}, u32[]{:S(2)}) collective-permute-start(bf16[96,576]{1,0:T(8,128)(2,1)S(1)} %pad_maximum_fusion.4), channel_id=1, source_target_pairs={{0,3},{1,0},{2,1},{3,2},{4,7},{5,4},{6,5},{7,6},{8,11},{9,8},{10,9... | collective-permute-start | bytes 331784 | tf_op jit(solution)/shard_map/ppermute | solution.py:451
  24.3 192.6 %all-gather.5.cloned.1.call-start = ((), (), s32[]{:S(2)}) async-start(), calls=%async_computation.2 | async-start | bytes 11943936 | tf_op jit(solution)/shard_map/all_gather | solution.py:466
  24.7 9.2 %collective-permute-start.7 = (bf16[96,1728]{1,0:T(8,128)(2,1)S(1)}, bf16[96,1728]{1,0:T(8,128)(2,1)S(1)}, u32[]{:S(2)}, u32[]{:S(2)}) collective-permute-start(bf16[96,1728]{1,0:T(8,128)(2,1)S(1)} %concatenate.59), channel_id=1, source_target_pairs={{0,1},{1,2},{2,3},{3,0},{4,5},{5,6},{6,7},{7,4},{8,9},{9,10},{10,1... | collective-permute-start | bytes 995336 | tf_op jit(solution)/shard_map/ppermute | solution.py:451
  24.8 29.3 %collective-permute-start.8 = (bf16[96,1728]{1,0:T(8,128)(2,1)S(1)}, bf16[96,1728]{1,0:T(8,128)(2,1)S(1)}, u32[]{:S(2)}, u32[]{:S(2)}) collective-permute-start(bf16[96,1728]{1,0:T(8,128)(2,1)S(1)} %concatenate.59), channel_id=1, source_target_pairs={{0,2},{1,3},{2,0},{3,1},{4,6},{5,7},{6,4},{7,5},{8,10},{9,11},{10,... | collective-permute-start | bytes 995336 | tf_op jit(solution)/shard_map/ppermute | solution.py:451
  25.4 30.8 %collective-permute-start.9 = (bf16[96,1728]{1,0:T(8,128)(2,1)S(1)}, bf16[96,1728]{1,0:T(8,128)(2,1)S(1)}, u32[]{:S(2)}, u32[]{:S(2)}) collective-permute-start(bf16[96,1728]{1,0:T(8,128)(2,1)S(1)} %concatenate.59), channel_id=1, source_target_pairs={{0,3},{1,0},{2,1},{3,2},{4,7},{5,4},{6,5},{7,6},{8,11},{9,8},{10,9... | collective-permute-start | bytes 995336 | tf_op jit(solution)/shard_map/ppermute | solution.py:451
  59.7 23.6 %copy-start.27 = (bf16[768]{0:T(1024)(128)(2,1)S(1)}, bf16[768]{0:T(1024)(128)(2,1)}, u32[]{:S(2)}) copy-start(bf16[768]{0:T(1024)(128)(2,1)} %param.39) | copy-start | bytes 4612
  59.7 23.6 %copy-start.28 = (bf16[768]{0:T(1024)(128)(2,1)S(1)}, bf16[768]{0:T(1024)(128)(2,1)}, u32[]{:S(2)}) copy-start(bf16[768]{0:T(1024)(128)(2,1)} %param.40) | copy-start | bytes 4612
  59.7 23.6 %copy-start.23 = (bf16[3072]{0:T(1024)(128)(2,1)S(1)}, bf16[3072]{0:T(1024)(128)(2,1)}, u32[]{:S(2)}) copy-start(bf16[3072]{0:T(1024)(128)(2,1)} %param.37) | copy-start | bytes 18436
  59.7 23.6 %copy-start.29 = (bf16[768]{0:T(1024)(128)(2,1)S(1)}, bf16[768]{0:T(1024)(128)(2,1)}, u32[]{:S(2)}) copy-start(bf16[768]{0:T(1024)(128)(2,1)} %param.38) | copy-start | bytes 4612
  59.8 23.6 %copy-start.15 = (bf16[768,768]{1,0:T(8,128)(2,1)S(1)}, bf16[768,768]{1,0:T(8,128)(2,1)}, u32[]{:S(2)}) copy-start(bf16[768,768]{1,0:T(8,128)(2,1)} %param.43) | copy-start | bytes 3538948
  59.8 385.6 %reduce-scatter.2.cloned.1.call-start = ((), (), s32[]{:S(2)}) async-start(), calls=%async_computation.3 | async-start | bytes 13713408 | tf_op jit(solution)/shard_map/reduce_scatter | solution.py:492
  59.8 46.0 %collective-permute-start.4 = (bf16[768,768]{1,0:T(8,128)(2,1)S(1)}, bf16[768,768]{1,0:T(8,128)(2,1)}, u32[]{:S(2)}, u32[]{:S(2)}) collective-permute-start(bf16[768,768]{1,0:T(8,128)(2,1)S(1)} %copy-done.12), channel_id=1, source_target_pairs={{0,1},{1,2},{2,3},{4,5},{5,6},{6,7},{8,9},{9,10},{10,11},{12,13},{... | collective-permute-start | bytes 3538952 | tf_op jit(solution)/shard_map/ppermute | solution.py:549
  61.9 47.4 %collective-permute-start.5 = (bf16[768,768]{1,0:T(8,128)(2,1)S(1)}, bf16[768,768]{1,0:T(8,128)(2,1)}, u32[]{:S(2)}, u32[]{:S(2)}) collective-permute-start(bf16[768,768]{1,0:T(8,128)(2,1)S(1)} %copy-done.12), channel_id=1, source_target_pairs={{1,0},{2,1},{3,2},{5,4},{6,5},{7,6},{9,8},{10,9},{11,10},{13,12},{... | collective-permute-start | bytes 3538952 | tf_op jit(solution)/shard_map/ppermute | solution.py:549
  67.2 36.8 %collective-permute-start.3 = (bf16[256,768]{1,0:T(8,128)(2,1)}, bf16[256,768]{1,0:T(8,128)(2,1)}, u32[]{:S(2)}, u32[]{:S(2)}) collective-permute-start(bf16[256,768]{1,0:T(8,128)(2,1)} %get-tuple-element.219), channel_id=1, source_target_pairs={{0,2},{1,3},{4,6},{5,7},{8,10},{9,11},{12,14},{13,15},{16,18},{17,... | collective-permute-start | bytes 1179656 | tf_op jit(solution)/shard_map/ppermute | solution.py:549
  70.9 40.8 %collective-permute-start.6 = (bf16[256,768]{1,0:T(8,128)(2,1)}, bf16[256,768]{1,0:T(8,128)(2,1)S(1)}, u32[]{:S(2)}, u32[]{:S(2)}) collective-permute-start(bf16[256,768]{1,0:T(8,128)(2,1)} %get-tuple-element.218), channel_id=1, source_target_pairs={{2,0},{3,1},{6,4},{7,5},{10,8},{11,9},{14,12},{15,13},{18,16},{19,... | collective-permute-start | bytes 1179656 | tf_op jit(solution)/shard_map/ppermute | solution.py:549
  83.3 47.9 %copy-start = (s32[768,1]{1,0:T(8,128)}, s32[768,1]{1,0:T(8,128)S(1)}, u32[]{:S(2)}) copy-start(s32[768,1]{1,0:T(8,128)S(1)} %reshape.539.qs_ref) | copy-start | bytes 9220
  476.1 64.3 %collective-permute-start.20 = (f32[96,1968]{1,0:T(8,128)}, f32[96,1968]{1,0:T(8,128)}, u32[]{:S(2)}, u32[]{:S(2)}) collective-permute-start(f32[96,1968]{1,0:T(8,128)} %get-tuple-element.162), channel_id=1, source_target_pairs={{0,1},{1,2},{2,3},{3,0},{4,5},{5,6},{6,7},{7,4},{8,9},{9,10},{10,1... | collective-permute-start | bytes 2267144 | tf_op jit(solution)/shard_map/ppermute | solution.py:527
  476.1 66.2 %collective-permute-start.21 = (f32[96,1968]{1,0:T(8,128)}, f32[96,1968]{1,0:T(8,128)}, u32[]{:S(2)}, u32[]{:S(2)}) collective-permute-start(f32[96,1968]{1,0:T(8,128)} %get-tuple-element.164), channel_id=1, source_target_pairs={{0,2},{1,3},{2,0},{3,1},{4,6},{5,7},{6,4},{7,5},{8,10},{9,11},{10,... | collective-permute-start | bytes 2267144 | tf_op jit(solution)/shard_map/ppermute | solution.py:527
  476.1 67.5 %collective-permute-start.22 = (f32[96,1968]{1,0:T(8,128)}, f32[96,1968]{1,0:T(8,128)}, u32[]{:S(2)}, u32[]{:S(2)}) collective-permute-start(f32[96,1968]{1,0:T(8,128)} %get-tuple-element.163), channel_id=1, source_target_pairs={{0,3},{1,0},{2,1},{3,2},{4,7},{5,4},{6,5},{7,6},{8,11},{9,8},{10,9... | collective-permute-start | bytes 2267144 | tf_op jit(solution)/shard_map/ppermute | solution.py:527
  505.4 30.6 %collective-permute-start.14 = (bf16[4,96,2496]{2,1,0:T(8,128)(2,1)}, bf16[4,96,2496]{2,1,0:T(8,128)(2,1)}, u32[]{:S(2)}, u32[]{:S(2)}) collective-permute-start(bf16[4,96,2496]{2,1,0:T(8,128)(2,1)} %fusion.32), channel_id=1, source_target_pairs={{0,4},{4,0},{8,12},{12,8},{16,20},{20,16},{24,28},{28,24},{1,5},{5... | collective-permute-start | bytes 5750792 | tf_op jit(solution)/shard_map/ppermute | solution.py:507
  532.0 58.4 %collective-permute-start.10 = (bf16[768,768]{0,1:T(8,128)(2,1)}, bf16[768,768]{0,1:T(8,128)(2,1)}, u32[]{:S(2)}, u32[]{:S(2)}) collective-permute-start(bf16[768,768]{0,1:T(8,128)(2,1)} %get-tuple-element.160), channel_id=1, source_target_pairs={{1,0},{2,1},{3,2},{5,4},{6,5},{7,6},{9,8},{10,9},{11,10},{13,12},{... | collective-permute-start | bytes 3538952 | tf_op jit(solution)/shard_map/ppermute | solution.py:549
  539.3 22.7 %collective-permute-start.15 = (bf16[2,96,2496]{2,1,0:T(8,128)(2,1)S(1)}, bf16[2,96,2496]{2,1,0:T(8,128)(2,1)S(1)}, u32[]{:S(2)}, u32[]{:S(2)}) collective-permute-start(bf16[2,96,2496]{2,1,0:T(8,128)(2,1)S(1)} %fusion.54), channel_id=1, source_target_pairs={{0,8},{4,12},{8,0},{12,4},{16,24},{20,28},{24,16},{28,20},{1,9},{5... | collective-permute-start | bytes 2875400 | tf_op jit(solution)/shard_map/ppermute | solution.py:507
  540.4 50.0 %collective-permute-start.12 = (bf16[768,768]{0,1:T(8,128)(2,1)}, bf16[768,768]{0,1:T(8,128)(2,1)}, u32[]{:S(2)}, u32[]{:S(2)}) collective-permute-start(bf16[768,768]{0,1:T(8,128)(2,1)} %get-tuple-element.161), channel_id=1, source_target_pairs={{0,1},{1,2},{2,3},{4,5},{5,6},{6,7},{8,9},{9,10},{10,11},{12,13},{... | collective-permute-start | bytes 3538952 | tf_op jit(solution)/shard_map/ppermute | solution.py:549
  542.3 45.3 %collective-permute-start.11 = (bf16[256,768]{0,1:T(8,128)(2,1)}, bf16[256,768]{0,1:T(8,128)(2,1)}, u32[]{:S(2)}, u32[]{:S(2)}) collective-permute-start(bf16[256,768]{0,1:T(8,128)(2,1)} %get-tuple-element.158), channel_id=1, source_target_pairs={{2,0},{3,1},{6,4},{7,5},{10,8},{11,9},{14,12},{15,13},{18,16},{19,... | collective-permute-start | bytes 1179656 | tf_op jit(solution)/shard_map/ppermute | solution.py:549
  543.6 46.0 %collective-permute-start.13 = (bf16[256,768]{0,1:T(8,128)(2,1)}, bf16[256,768]{0,1:T(8,128)(2,1)}, u32[]{:S(2)}, u32[]{:S(2)}) collective-permute-start(bf16[256,768]{0,1:T(8,128)(2,1)} %get-tuple-element.159), channel_id=1, source_target_pairs={{0,2},{1,3},{4,6},{5,7},{8,10},{9,11},{12,14},{13,15},{16,18},{17,... | collective-permute-start | bytes 1179656 | tf_op jit(solution)/shard_map/ppermute | solution.py:549
  564.4 11.6 %collective-permute-start.16 = (bf16[1,96,2496]{2,1,0:T(8,128)(2,1)}, bf16[1,96,2496]{2,1,0:T(8,128)(2,1)}, u32[]{:S(2)}, u32[]{:S(2)}) collective-permute-start(bf16[1,96,2496]{2,1,0:T(8,128)(2,1)} %dynamic-slice_convert_fusion.2), channel_id=1, source_target_pairs={{0,16},{4,20},{8,24},{12,28},{16,0},{20,4},{24,8},{28,12},{1,17},{... | collective-permute-start | bytes 1437704 | tf_op jit(solution)/shard_map/ppermute | solution.py:507
  587.6 11.4 %collective-permute-start.17 = (f32[96,624]{1,0:T(8,128)}, f32[96,624]{1,0:T(8,128)}, u32[]{:S(2)}, u32[]{:S(2)}) collective-permute-start(f32[96,624]{1,0:T(8,128)} %get-tuple-element.220), channel_id=1, source_target_pairs={{0,1},{1,2},{2,3},{3,0},{4,5},{5,6},{6,7},{7,4},{8,9},{9,10},{10,1... | collective-permute-start | bytes 718856 | tf_op jit(solution)/shard_map/ppermute | solution.py:527
  587.6 19.3 %collective-permute-start.18 = (f32[96,624]{1,0:T(8,128)}, f32[96,624]{1,0:T(8,128)}, u32[]{:S(2)}, u32[]{:S(2)}) collective-permute-start(f32[96,624]{1,0:T(8,128)} %get-tuple-element.222), channel_id=1, source_target_pairs={{0,2},{1,3},{2,0},{3,1},{4,6},{5,7},{6,4},{7,5},{8,10},{9,11},{10,... | collective-permute-start | bytes 718856 | tf_op jit(solution)/shard_map/ppermute | solution.py:527
  589.6 22.6 %collective-permute-start.19 = (f32[96,624]{1,0:T(8,128)}, f32[96,624]{1,0:T(8,128)}, u32[]{:S(2)}, u32[]{:S(2)}) collective-permute-start(f32[96,624]{1,0:T(8,128)} %get-tuple-element.221), channel_id=1, source_target_pairs={{0,3},{1,0},{2,1},{3,2},{4,7},{5,4},{6,5},{7,6},{8,11},{9,8},{10,9... | collective-permute-start | bytes 718856 | tf_op jit(solution)/shard_map/ppermute | solution.py:527
  (31 other events, 220.8 us)
Sparse Core Ops, SparseCore 0:
  24.4 34.2 all-gather.2
  61.2 63.6 all-gather.4
  332.6 86.7 reduce-scatter.1
where the time goes:
time: 631 us; the launch traced here: 621 us
  Pallas kernels  183 us (29%)
  matrix products  137 us (22%)
  local copies, waits for them, and re-layouts  118 us (19%)
  waiting for transfers between devices  88.8 us (14%)
  starting transfers between devices  40.8 us (6%)
  other arithmetic  38.9 us (6%)
  between operations  14.9 us (2%)
    pallas_call x1, Pallas kernels, flash_backward(): pl.pallas_call(_attn_bwd, grid_spec=grid_spec, cost_estimate=pl.CostEstim...  97.4 us
    pallas_call x1, Pallas kernels, flash_forward(): pl.pallas_call(_attn_fwd, grid_spec=grid_spec, cost_estimate=pl.CostEstim...  85.7 us
    dot_general x6, matrix products, contract_last(): lax.dot_general(left, right, (((1,), (1,)), ((), ())), preferred_element_...  41.6 us
    ppermute x6, waiting for transfers between devices, cyclic_pieces(): lax.ppermute(piece, 'tensor', [(s, (s + k) % count) for s in range(count)])  38.9 us
    dot_general x6, matrix products, contract_first(): lax.dot_general(left, right, (((0,), (0,)), ((), ())), preferred_element_...  30.1 us
    concatenate x7, local copies, waits for them, and re-layouts, pack_grads(): cat = jnp.concatenate(mats, axis=1)  29.7 us
    dot_general x1, matrix products, shards(): jnp.dot(hidden_low, wi, preferred_element_type=jnp.float32)  29.6 us
    unnamed x84, local copies, waits for them, and re-layouts  28.3 us
  transfers between devices with their start and end apart: 26, of which 10 were waited for; matrix products, arithmetic and copies ran while one was open for 22% of the time, Pallas kernels for 29%

commit v1 on v0

--- a/solution.py
+++ b/solution.py
@@ -554,6 +554,34 @@
     left = [shift_rows(own[rows - take:], d + 1, count) for d, take in enumerate(takes)]
     right = [shift_rows(own[:take], -(d + 1), count) for d, take in enumerate(takes)]
     return jnp.concatenate(left[::-1] + [own] + right, axis=0)
+
+
+def return_halo(left_vals, right_vals, takes, count):
+    rows = None
+    backs = []
+    at = left_vals.shape[0]
+    for d, take in enumerate(takes):
+        piece = left_vals[at - take:at].astype(jnp.bfloat16)
+        at -= take
+        backs.append(("last", shift_rows(piece, -(d + 1), count)))
+    at = 0
+    for d, take in enumerate(takes):
+        piece = right_vals[at:at + take].astype(jnp.bfloat16)
+        at += take
+        backs.append(("first", shift_rows(piece, d + 1, count)))
+    return backs
+
+
+def add_backs(total, backs):
+    rows = total.shape[0]
+    for where_to, got in backs:
+        take = got.shape[0]
+        got = got.astype(jnp.float32)
+        if where_to == "last":
+            total = total + jnp.pad(got, ((rows - take, 0), (0, 0)))
+        else:
+            total = total + jnp.pad(got, ((0, rows - take), (0, 0)))
+    return total
 
 
 def return_window(values, takes, count):
@@ -666,8 +694,11 @@
     grad_query_w = contract_first(x_own, grad_query)
     grad_key_w = contract_first(x_win, grad_key)
     grad_value_w = contract_first(x_win, grad_value)
-    grad_win = contract_last(grad_key, wk) + contract_last(grad_value, wv)
-    grad_tokens = grad_resid_one + contract_last(grad_query, wq) + return_window(grad_win, takes, count)
+    halo = sum(takes)
+    def win_grad(lo_row, hi_row):
+        return contract_last(grad_key[lo_row:hi_row], wk) + contract_last(grad_value[lo_row:hi_row], wv)
+    back = return_halo(win_grad(0, halo), win_grad(halo + rows, 2 * halo + rows), takes, count)
+    grad_tokens = add_backs(grad_resid_one + contract_last(grad_query, wq) + win_grad(halo, halo + rows), back)
 
     late_widths, late_cat = pack_grads(
         [grad_query_w, grad_key_w, grad_value_w], [column_sum(grad_query), column_sum(grad_value)]

time: 631 us -> 669 us (1.060)
  the two profiles are of different devices: /device:TPU:9 before, /device:TPU:4 now
where the time goes in v1:
time: 669 us; the launch traced here: 657 us
  Pallas kernels  150 us (22%)
  matrix products  136 us (20%)
  starting transfers between devices  119 us (18%)
  local copies, waits for them, and re-layouts  116 us (17%)
  waiting for transfers between devices  84 us (13%)
  other arithmetic  37.5 us (6%)
  between operations  15 us (2%)
    pallas_call x1, Pallas kernels, flash_backward(): pl.pallas_call(_attn_bwd, grid_spec=grid_spec, cost_estimate=pl.CostEstim...  85.8 us
    pallas_call x1, Pallas kernels, flash_forward(): pl.pallas_call(_attn_fwd, grid_spec=grid_spec, cost_estimate=pl.CostEstim...  64.5 us
    ppermute x8, starting transfers between devices, shift_rows(): return lax.ppermute(values, 'tensor', pairs)  61.6 us
    ppermute x6, starting transfers between devices, reduce_tensor(): lax.ppermute(send, 'tensor', [(s, (s + k) % count) for s in range(count)])  41.7 us
    dot_general x10, matrix products, contract_last(): lax.dot_general(left, right, (((1,), (1,)), ((), ())), preferred_element_...  36.7 us
    dot_general x6, matrix products, contract_first(): lax.dot_general(left, right, (((0,), (0,)), ((), ())), preferred_element_...  34 us
    concatenate x7, local copies, waits for them, and re-layouts, pack_grads(): cat = jnp.concatenate(mats, axis=1)  29.7 us
    dot_general x1, matrix products, shards(): jnp.dot(hidden_low, wi, preferred_element_type=jnp.float32)  29.7 us
  transfers between devices with their start and end apart: 26, of which 10 were waited for; matrix products, arithmetic and copies ran while one was open for 16% of the time, Pallas kernels for 23%

profile of v1, /device:TPU:4, one launch (start us, length us, event | category | flops | bytes accessed | tf_op | source)
XLA Modules:
  0.0 657.2 jit_solution(9576168986713107662)
XLA Ops:
  16.3 4.2 collective-permute-done.1
  28.6 7.7 %collective-permute-done.7 = bf16[96,1728]{1,0:T(8,128)(2,1)S(1)} collective-permute-done((bf16[96,1728]{1,0:T(8,128)(2,1)S(1)}, bf16[96,1728]{1,0:T(8,128)(2,1)S(1)}, u32[]{:S(2)}, u32[]{:S(2)}) %collective-permute-start.7) | collective-permute-done | bytes 331808 | tf_op jit(solution)/shard_map/ppermute | solution.py:451
  36.3 13.3 %collective-permute-done.8 = bf16[96,1728]{1,0:T(8,128)(2,1)S(1)} collective-permute-done((bf16[96,1728]{1,0:T(8,128)(2,1)S(1)}, bf16[96,1728]{1,0:T(8,128)(2,1)S(1)}, u32[]{:S(2)}, u32[]{:S(2)}) %collective-permute-start.8) | collective-permute-done | bytes 331808 | tf_op jit(solution)/shard_map/ppermute | solution.py:451
  53.3 10.9 %collective-permute-start.4 = (bf16[768,768]{1,0:T(8,128)(2,1)S(1)}, bf16[768,768]{1,0:T(8,128)(2,1)}, u32[]{:S(2)}, u32[]{:S(2)}) collective-permute-start(bf16[768,768]{1,0:T(8,128)(2,1)S(1)} %copy-done.11), channel_id=1, source_target_pairs={{0,1},{1,2},{2,3},{4,5},{5,6},{6,7},{8,9},{9,10},{10,11},{12,13},{... | collective-permute-start | bytes 3538952 | tf_op jit(solution)/shard_map/ppermute | solution.py:549
  66.4 4.2 collective-permute-start.3
  85.7 11.5 %collective-permute-done.3 = bf16[256,768]{1,0:T(8,128)(2,1)} collective-permute-done((bf16[256,768]{1,0:T(8,128)(2,1)}, bf16[256,768]{1,0:T(8,128)(2,1)}, u32[]{:S(2)}, u32[]{:S(2)}) %collective-permute-start.3) | collective-permute-done | bytes 393248 | tf_op jit(solution)/shard_map/ppermute | solution.py:549
  104.9 4.4 collective-permute-done.6
  112.7 8.2 %convolution_convert_fusion.2.k_ref = bf16[2816,768]{1,0:T(8,128)(2,1)} fusion(bf16[2816,768]{1,0:T(8,128)(2,1)} %constant_dynamic-update-slice_fusion, bf16[768,2304]{1,0:T(8,128)(2,1)S(1)} %copy-done.19), kind=kOutput, calls=%fused_computation.22 | convolution fusion | flops 3324051456 | bytes 9830400 | tf_op jit(solution)/shard_map/dot_general | solution.py:645
  120.8 7.9 %add_convert_fusion.1.v_ref = bf16[2816,768]{1,0:T(8,128)(2,1)} fusion(bf16[2816,768]{1,0:T(8,128)(2,1)} %constant_dynamic-update-slice_fusion, f32[768]{0:T(1024)S(1)} %convert_element_type.221, bf16[768,2304]{1,0:T(8,128)(2,1)S(1)} %copy-done.19), kind=kOutput, calls=%fused_computation.19 | convolution fusion | flops 3326214144 | bytes 9834496 | tf_op jit(solution)/shard_map/dot_general | solution.py:646
  128.7 64.5 %shard_map.314 = (f32[768,768]{1,0:T(8,128)S(1)}, f32[12,768,1]{2,1,0:T(8,128)}) custom-call(s32[3]{0:T(128)S(1)} %fusion.79.lo_ref, s32[3]{0:T(128)S(1)} %fusion.78.hi_ref, bf16[768,768]{1,0:T(8,128)(2,1)S(1)} %fusion.37.q_ref, bf16[2816,768]{1,0:T(8,128)(2,1)} %convolution_convert_fusion.2.k_ref, bf16[2816,768]{1,0:T(8,128)(2,1)} %add_convert_fusion.1.v_ref, ...), custom_call_target="tpu_custom_call" | custom-call | flops 4831838208 | bytes 19660800 | tf_op jit(solution)/shard_map/pallas_call | solution.py:275
  196.3 29.7 %multiply_convert_fusion = (bf16[768,3072]{1,0:T(8,128)(2,1)S(1)}, f32[768,3072]{1,0:T(8,128)}, f32[768,3072]{1,0:T(8,128)}) fusion(f32[3072]{0:T(1024)S(1)} %convert_element_type.229, bf16[768,6912]{1,0:T(8,128)(2,1)} %all-gather.5.cloned.1.call-done, f32[768,768]{0,1:T(8,128)S(1)} %get-tuple-element.277, f32[768]{0:T(1024)S(1)} %convert_element_type.227, ...), kind=kOutput, calls=%fused_computation.5 | convolution fusion | flops 3782541312 | bytes 30695424 | tf_op jit(solution)/shard_map/dot_general | solution.py:653
  226.0 6.0 fusion.102
  237.6 5.5 convolution_convert_fusion
  243.1 13.7 %fusion.103 = (bf16[3072]{0:T(1024)(128)(2,1)}, bf16[768,3072]{1,0:T(8,128)(2,1)S(1)}) fusion(f32[768,3072]{1,0:T(8,128)} %get-tuple-element.152, bf16[768,768]{0,1:T(8,128)(2,1)S(1)} %get-tuple-element.148, bf16[768,6912]{1,0:T(8,128)(2,1)} %all-gather.5.cloned.1.call-done, f32[768,3072]{1,0:T(8,128)} %get-tuple-element.278, ...), kind=kOutput, calls=%fused_computation.253 | convolution fusion | flops 3661624320 | bytes 29509632 | tf_op jit(solution)/shard_map/dot_general | solution.py:662
  256.8 5.8 convolution_convert_fusion.1
  262.7 7.9 %multiply_reduce_fusion = (bf16[768]{0:T(1024)(128)(2,1)}, f32[768]{0:T(1024)S(1)}, f32[768]{0:T(1024)S(1)}, bf16[768]{0:T(1024)(128)(2,1)}, f32[768,768]{0,1:T(8,128)S(1)}) fusion(f32[768,768]{0,1:T(8,128)S(1)} %get-tuple-element.277, f32[768]{0:T(1024)S(1)} %add_rsqrt_fusion.1, f32[768]{0:T(1024)S(1)} %broadcast_multiply_fusion.5, ...), kind=kOutput, calls=%fused_computation.47 | convolution fusion | flops 3634492416 | bytes 17728512 | tf_op jit(solution)/shard_map/dot_general | solution.py:424
  287.4 18.3 %concatenate.61 = bf16[768,7872]{1,0:T(8,128)(2,1)} concatenate(bf16[768,768]{1,0:T(8,128)(2,1)S(1)} %copy.133, bf16[768,3072]{1,0:T(8,128)(2,1)} %convolution_convert_fusion.1, bf16[768,3072]{1,0:T(8,128)(2,1)} %convolution_convert_fusion, bf16[768,96]{1,0:T(8,128)(2,1)} %bitcast.196, bf16[768,384]{1,0:T(8,128)(2,1)} %bitcast.186, bf16[768,96]{1,0:T(8,128)(2,1)} %bitcast.199, ...), dimensions={1} | concatenate | bytes 24182784 | tf_op jit(solution)/shard_map/concatenate | solution.py:487
  322.8 85.8 %shard_map.315 = (f32[2816,768]{1,0:T(8,128)}, f32[2816,768]{1,0:T(8,128)}, f32[768,768]{1,0:T(8,128)S(1)}) custom-call(s32[11]{0:T(128)S(1)} %copy-done.2, s32[11]{0:T(128)S(1)} %get-tuple-element.143.hi_ref, bf16[768,768]{1,0:T(8,128)(2,1)S(1)} %copy-done.4, bf16[2816,768]{1,0:T(8,128)(2,1)} %convolution_convert_fusion.2.k_ref, ...), custom_call_target="tpu_custom_call" | custom-call | flops 12079595520 | bytes 39321600 | tf_op jit(solution)/shard_map/pallas_call | solution.py:374
  408.6 13.6 %reduce-scatter.2.cloned.1.call-done = bf16[96,7872]{1,0:T(8,128)(2,1)} async-done(((bf16[768,7872]{1,0:T(8,128)(2,1)}), bf16[96,7872]{1,0:T(8,128)(2,1)}) %reduce-scatter.2.cloned.1.call-update) | async-done | bytes 1511440 | tf_op jit(solution)/shard_map/reduce_scatter | solution.py:492
  429.4 9.0 %convolution_convert_fusion.3 = bf16[768,768]{1,0:T(8,128)(2,1)} fusion(bf16[2816,768]{1,0:T(8,128)(2,1)} %constant_dynamic-update-slice_fusion, bf16[2816,768]{1,0:T(8,128)(2,1)} %get-tuple-element.146), kind=kOutput, calls=%fused_computation.71 | convolution fusion | flops 3322478592 | bytes 9830400 | tf_op jit(solution)/shard_map/dot_general | solution.py:428
  438.9 7.8 %convolution_convert_fusion.4 = bf16[768,768]{1,0:T(8,128)(2,1)S(1)} fusion(bf16[2816,768]{1,0:T(8,128)(2,1)} %constant_dynamic-update-slice_fusion, bf16[2816,768]{1,0:T(8,128)(2,1)S(1)} %convert_element_type.251), kind=kOutput, calls=%fused_computation.72 | convolution fusion | flops 3322478592 | bytes 9830400 | tf_op jit(solution)/shard_map/dot_general | solution.py:428
  463.5 6.5 concatenate.67
  494.0 17.0 %collective-permute-start.20 = (f32[96,1968]{1,0:T(8,128)S(1)}, f32[96,1968]{1,0:T(8,128)S(1)}, u32[]{:S(2)}, u32[]{:S(2)}) collective-permute-start(f32[96,1968]{1,0:T(8,128)S(1)} %get-tuple-element.160), channel_id=1, source_target_pairs={{0,1},{1,2},{2,3},{3,0},{4,5},{5,6},{6,7},{7,4},{8,9},{9,10},{10,1... | collective-permute-start | bytes 2267144 | tf_op jit(solution)/shard_map/ppermute | solution.py:527
  511.0 5.3 collective-permute-start.21
  520.4 3.8 fusion.38
  526.5 4.2 collective-permute-start.15
  535.8 15.7 %collective-permute-done.21 = f32[96,1968]{1,0:T(8,128)S(1)} collective-permute-done((f32[96,1968]{1,0:T(8,128)S(1)}, f32[96,1968]{1,0:T(8,128)S(1)}, u32[]{:S(2)}, u32[]{:S(2)}) %collective-permute-start.21) | collective-permute-done | bytes 755744 | tf_op jit(solution)/shard_map/ppermute | solution.py:527
  551.6 36.1 %collective-permute-start.12 = (bf16[768,768]{0,1:T(8,128)(2,1)}, bf16[768,768]{0,1:T(8,128)(2,1)}, u32[]{:S(2)}, u32[]{:S(2)}) collective-permute-start(bf16[768,768]{0,1:T(8,128)(2,1)} %slice.582), channel_id=1, source_target_pairs={{0,1},{1,2},{2,3},{4,5},{5,6},{6,7},{8,9},{9,10},{10,11},{12,13},{... | collective-permute-start | bytes 3538952 | tf_op jit(solution)/shard_map/ppermute | solution.py:549
  587.7 5.0 collective-permute-start.13
  598.2 9.5 %collective-permute-done.16 = bf16[1,96,2496]{2,1,0:T(8,128)(2,1)} collective-permute-done((bf16[1,96,2496]{2,1,0:T(8,128)(2,1)}, bf16[1,96,2496]{2,1,0:T(8,128)(2,1)}, u32[]{:S(2)}, u32[]{:S(2)}) %collective-permute-start.16) | collective-permute-done | bytes 479264 | tf_op jit(solution)/shard_map/ppermute | solution.py:507
  621.8 16.5 %collective-permute-start.19 = (f32[96,624]{1,0:T(8,128)}, f32[96,624]{1,0:T(8,128)}, u32[]{:S(2)}, u32[]{:S(2)}) collective-permute-start(f32[96,624]{1,0:T(8,128)} %get-tuple-element.219), channel_id=1, source_target_pairs={{0,3},{1,0},{2,1},{3,2},{4,7},{5,4},{6,5},{7,6},{8,11},{9,8},{10,9... | collective-permute-start | bytes 718856 | tf_op jit(solution)/shard_map/ppermute | solution.py:527
  638.3 6.5 convert_add_fusion
  (278 shorter events, 176.0 us)
Async XLA Ops:
  7.2 103.0 %all-gather.3.cloned.1.call-start = ((), (), s32[]{:S(2)}) async-start(), calls=%async_computation.1 | async-start | bytes 3981312 | tf_op jit(solution)/shard_map/all_gather | solution.py:466
  8.2 8.1 %collective-permute-start = (bf16[96,576]{1,0:T(8,128)(2,1)S(1)}, bf16[96,576]{1,0:T(8,128)(2,1)S(1)}, u32[]{:S(2)}, u32[]{:S(2)}) collective-permute-start(bf16[96,576]{1,0:T(8,128)(2,1)S(1)} %pad_maximum_fusion.4), channel_id=1, source_target_pairs={{0,1},{1,2},{2,3},{3,0},{4,5},{5,6},{6,7},{7,4},{8,9},{9,10},{10,1... | collective-permute-start | bytes 331784 | tf_op jit(solution)/shard_map/ppermute | solution.py:451
  9.8 10.7 %collective-permute-start.1 = (bf16[96,576]{1,0:T(8,128)(2,1)S(1)}, bf16[96,576]{1,0:T(8,128)(2,1)S(1)}, u32[]{:S(2)}, u32[]{:S(2)}) collective-permute-start(bf16[96,576]{1,0:T(8,128)(2,1)S(1)} %pad_maximum_fusion.4), channel_id=1, source_target_pairs={{0,2},{1,3},{2,0},{3,1},{4,6},{5,7},{6,4},{7,5},{8,10},{9,11},{10,... | collective-permute-start | bytes 331784 | tf_op jit(solution)/shard_map/ppermute | solution.py:451
  12.4 8.1 %collective-permute-start.2 = (bf16[96,576]{1,0:T(8,128)(2,1)S(1)}, bf16[96,576]{1,0:T(8,128)(2,1)S(1)}, u32[]{:S(2)}, u32[]{:S(2)}) collective-permute-start(bf16[96,576]{1,0:T(8,128)(2,1)S(1)} %pad_maximum_fusion.4), channel_id=1, source_target_pairs={{0,3},{1,0},{2,1},{3,2},{4,7},{5,4},{6,5},{7,6},{8,11},{9,8},{10,9... | collective-permute-start | bytes 331784 | tf_op jit(solution)/shard_map/ppermute | solution.py:451
  22.6 170.6 %all-gather.5.cloned.1.call-start = ((), (), s32[]{:S(2)}) async-start(), calls=%async_computation.2 | async-start | bytes 11943936 | tf_op jit(solution)/shard_map/all_gather | solution.py:466
  23.0 13.3 %collective-permute-start.7 = (bf16[96,1728]{1,0:T(8,128)(2,1)S(1)}, bf16[96,1728]{1,0:T(8,128)(2,1)S(1)}, u32[]{:S(2)}, u32[]{:S(2)}) collective-permute-start(bf16[96,1728]{1,0:T(8,128)(2,1)S(1)} %concatenate.59), channel_id=1, source_target_pairs={{0,1},{1,2},{2,3},{3,0},{4,5},{5,6},{6,7},{7,4},{8,9},{9,10},{10,1... | collective-permute-start | bytes 995336 | tf_op jit(solution)/shard_map/ppermute | solution.py:451
  26.2 23.5 %collective-permute-start.8 = (bf16[96,1728]{1,0:T(8,128)(2,1)S(1)}, bf16[96,1728]{1,0:T(8,128)(2,1)S(1)}, u32[]{:S(2)}, u32[]{:S(2)}) collective-permute-start(bf16[96,1728]{1,0:T(8,128)(2,1)S(1)} %concatenate.59), channel_id=1, source_target_pairs={{0,2},{1,3},{2,0},{3,1},{4,6},{5,7},{6,4},{7,5},{8,10},{9,11},{10,... | collective-permute-start | bytes 995336 | tf_op jit(solution)/shard_map/ppermute | solution.py:451
  27.8 21.8 %collective-permute-start.9 = (bf16[96,1728]{1,0:T(8,128)(2,1)S(1)}, bf16[96,1728]{1,0:T(8,128)(2,1)S(1)}, u32[]{:S(2)}, u32[]{:S(2)}) collective-permute-start(bf16[96,1728]{1,0:T(8,128)(2,1)S(1)} %concatenate.59), channel_id=1, source_target_pairs={{0,3},{1,0},{2,1},{3,2},{4,7},{5,4},{6,5},{7,6},{8,11},{9,8},{10,9... | collective-permute-start | bytes 995336 | tf_op jit(solution)/shard_map/ppermute | solution.py:451
  53.2 29.9 %copy-start.25 = (bf16[3072]{0:T(1024)(128)(2,1)S(1)}, bf16[3072]{0:T(1024)(128)(2,1)}, u32[]{:S(2)}) copy-start(bf16[3072]{0:T(1024)(128)(2,1)} %param.37) | copy-start | bytes 18436
  53.2 30.0 %copy-start.31 = (bf16[768]{0:T(1024)(128)(2,1)S(1)}, bf16[768]{0:T(1024)(128)(2,1)}, u32[]{:S(2)}) copy-start(bf16[768]{0:T(1024)(128)(2,1)} %param.38) | copy-start | bytes 4612
  53.2 30.0 %copy-start.13 = (bf16[768,768]{1,0:T(8,128)(2,1)S(1)}, bf16[768,768]{1,0:T(8,128)(2,1)}, u32[]{:S(2)}) copy-start(bf16[768,768]{1,0:T(8,128)(2,1)} %param.43) | copy-start | bytes 3538948
  53.2 368.9 %reduce-scatter.2.cloned.1.call-start = ((), (), s32[]{:S(2)}) async-start(), calls=%async_computation.3 | async-start | bytes 13713408 | tf_op jit(solution)/shard_map/reduce_scatter | solution.py:492
  53.3 45.7 %collective-permute-start.4 = (bf16[768,768]{1,0:T(8,128)(2,1)S(1)}, bf16[768,768]{1,0:T(8,128)(2,1)}, u32[]{:S(2)}, u32[]{:S(2)}) collective-permute-start(bf16[768,768]{1,0:T(8,128)(2,1)S(1)} %copy-done.11), channel_id=1, source_target_pairs={{0,1},{1,2},{2,3},{4,5},{5,6},{6,7},{8,9},{9,10},{10,11},{12,13},{... | collective-permute-start | bytes 3538952 | tf_op jit(solution)/shard_map/ppermute | solution.py:549
  64.2 38.3 %collective-permute-start.5 = (bf16[768,768]{1,0:T(8,128)(2,1)S(1)}, bf16[768,768]{1,0:T(8,128)(2,1)}, u32[]{:S(2)}, u32[]{:S(2)}) collective-permute-start(bf16[768,768]{1,0:T(8,128)(2,1)S(1)} %copy-done.11), channel_id=1, source_target_pairs={{1,0},{2,1},{3,2},{5,4},{6,5},{7,6},{9,8},{10,9},{11,10},{13,12},{... | collective-permute-start | bytes 3538952 | tf_op jit(solution)/shard_map/ppermute | solution.py:549
  66.4 30.8 %collective-permute-start.3 = (bf16[256,768]{1,0:T(8,128)(2,1)}, bf16[256,768]{1,0:T(8,128)(2,1)}, u32[]{:S(2)}, u32[]{:S(2)}) collective-permute-start(bf16[256,768]{1,0:T(8,128)(2,1)} %get-tuple-element.217), channel_id=1, source_target_pairs={{0,2},{1,3},{4,6},{5,7},{8,10},{9,11},{12,14},{13,15},{16,18},{17,... | collective-permute-start | bytes 1179656 | tf_op jit(solution)/shard_map/ppermute | solution.py:549
  70.7 38.7 %collective-permute-start.6 = (bf16[256,768]{1,0:T(8,128)(2,1)}, bf16[256,768]{1,0:T(8,128)(2,1)S(1)}, u32[]{:S(2)}, u32[]{:S(2)}) collective-permute-start(bf16[256,768]{1,0:T(8,128)(2,1)} %get-tuple-element.216), channel_id=1, source_target_pairs={{2,0},{3,1},{6,4},{7,5},{10,8},{11,9},{14,12},{15,13},{18,16},{19,... | collective-permute-start | bytes 1179656 | tf_op jit(solution)/shard_map/ppermute | solution.py:549
  83.1 45.7 %copy-start = (s32[768,1]{1,0:T(8,128)}, s32[768,1]{1,0:T(8,128)S(1)}, u32[]{:S(2)}) copy-start(s32[768,1]{1,0:T(8,128)S(1)} %reshape.539.qs_ref) | copy-start | bytes 9220
  477.7 46.5 %collective-permute-start.14 = (bf16[4,96,2496]{2,1,0:T(8,128)(2,1)}, bf16[4,96,2496]{2,1,0:T(8,128)(2,1)}, u32[]{:S(2)}, u32[]{:S(2)}) collective-permute-start(bf16[4,96,2496]{2,1,0:T(8,128)(2,1)} %fusion.24), channel_id=1, source_target_pairs={{0,4},{4,0},{8,12},{12,8},{16,20},{20,16},{24,28},{28,24},{1,5},{5... | collective-permute-start | bytes 5750792 | tf_op jit(solution)/shard_map/ppermute | solution.py:507
  491.7 32.6 %slice-start = ((s8[7864320]{0:T(1024)(128)(4,1)}), s8[4194304]{0:T(1024)(128)(4,1)S(1)}, s32[]{:S(2)}) async-start(s8[7864320]{0:T(1024)(128)(4,1)} %bitcast.173), calls=%async_computation.4 | async-start | bytes 8388608
  493.7 30.6 %slice-start.1 = ((s8[7864320]{0:T(1024)(128)(4,1)}), s8[3670016]{0:T(1024)(128)(4,1)S(1)}, s32[]{:S(2)}) async-start(s8[7864320]{0:T(1024)(128)(4,1)} %bitcast.173), calls=%async_computation.5 | async-start | bytes 7340032
  494.0 40.6 %collective-permute-start.20 = (f32[96,1968]{1,0:T(8,128)S(1)}, f32[96,1968]{1,0:T(8,128)S(1)}, u32[]{:S(2)}, u32[]{:S(2)}) collective-permute-start(f32[96,1968]{1,0:T(8,128)S(1)} %get-tuple-element.160), channel_id=1, source_target_pairs={{0,1},{1,2},{2,3},{3,0},{4,5},{5,6},{6,7},{7,4},{8,9},{9,10},{10,1... | collective-permute-start | bytes 2267144 | tf_op jit(solution)/shard_map/ppermute | solution.py:527
  511.0 40.6 %collective-permute-start.21 = (f32[96,1968]{1,0:T(8,128)S(1)}, f32[96,1968]{1,0:T(8,128)S(1)}, u32[]{:S(2)}, u32[]{:S(2)}) collective-permute-start(f32[96,1968]{1,0:T(8,128)S(1)} %get-tuple-element.162), channel_id=1, source_target_pairs={{0,2},{1,3},{2,0},{3,1},{4,6},{5,7},{6,4},{7,5},{8,10},{9,11},{10,... | collective-permute-start | bytes 2267144 | tf_op jit(solution)/shard_map/ppermute | solution.py:527
  516.3 71.4 %collective-permute-start.22 = (f32[96,1968]{1,0:T(8,128)S(1)}, f32[96,1968]{1,0:T(8,128)S(1)}, u32[]{:S(2)}, u32[]{:S(2)}) collective-permute-start(f32[96,1968]{1,0:T(8,128)S(1)} %get-tuple-element.161), channel_id=1, source_target_pairs={{0,3},{1,0},{2,1},{3,2},{4,7},{5,4},{6,5},{7,6},{8,11},{9,8},{10,9... | collective-permute-start | bytes 2267144 | tf_op jit(solution)/shard_map/ppermute | solution.py:527
  519.1 119.1 %collective-permute-start.10 = (bf16[768,768]{0,1:T(8,128)(2,1)}, bf16[768,768]{0,1:T(8,128)(2,1)}, u32[]{:S(2)}, u32[]{:S(2)}) collective-permute-start(bf16[768,768]{0,1:T(8,128)(2,1)} %slice.578), channel_id=1, source_target_pairs={{1,0},{2,1},{3,2},{5,4},{6,5},{7,6},{9,8},{10,9},{11,10},{13,12},{... | collective-permute-start | bytes 3538952 | tf_op jit(solution)/shard_map/ppermute | solution.py:549
  526.5 66.4 %collective-permute-start.15 = (bf16[2,96,2496]{2,1,0:T(8,128)(2,1)S(1)}, bf16[2,96,2496]{2,1,0:T(8,128)(2,1)S(1)}, u32[]{:S(2)}, u32[]{:S(2)}) collective-permute-start(bf16[2,96,2496]{2,1,0:T(8,128)(2,1)S(1)} %fusion.49), channel_id=1, source_target_pairs={{0,8},{4,12},{8,0},{12,4},{16,24},{20,28},{24,16},{28,20},{1,9},{5... | collective-permute-start | bytes 2875400 | tf_op jit(solution)/shard_map/ppermute | solution.py:507
  534.5 84.8 %collective-permute-start.11 = (bf16[256,768]{0,1:T(8,128)(2,1)}, bf16[256,768]{0,1:T(8,128)(2,1)}, u32[]{:S(2)}, u32[]{:S(2)}) collective-permute-start(bf16[256,768]{0,1:T(8,128)(2,1)} %slice.579), channel_id=1, source_target_pairs={{2,0},{3,1},{6,4},{7,5},{10,8},{11,9},{14,12},{15,13},{18,16},{19,... | collective-permute-start | bytes 1179656 | tf_op jit(solution)/shard_map/ppermute | solution.py:549
  551.6 86.7 %collective-permute-start.12 = (bf16[768,768]{0,1:T(8,128)(2,1)}, bf16[768,768]{0,1:T(8,128)(2,1)}, u32[]{:S(2)}, u32[]{:S(2)}) collective-permute-start(bf16[768,768]{0,1:T(8,128)(2,1)} %slice.582), channel_id=1, source_target_pairs={{0,1},{1,2},{2,3},{4,5},{5,6},{6,7},{8,9},{9,10},{10,11},{12,13},{... | collective-permute-start | bytes 3538952 | tf_op jit(solution)/shard_map/ppermute | solution.py:549
  587.7 34.1 %collective-permute-start.13 = (bf16[256,768]{0,1:T(8,128)(2,1)}, bf16[256,768]{0,1:T(8,128)(2,1)}, u32[]{:S(2)}, u32[]{:S(2)}) collective-permute-start(bf16[256,768]{0,1:T(8,128)(2,1)} %slice.583), channel_id=1, source_target_pairs={{0,2},{1,3},{4,6},{5,7},{8,10},{9,11},{12,14},{13,15},{16,18},{17,... | collective-permute-start | bytes 1179656 | tf_op jit(solution)/shard_map/ppermute | solution.py:549
  595.3 12.5 %collective-permute-start.16 = (bf16[1,96,2496]{2,1,0:T(8,128)(2,1)}, bf16[1,96,2496]{2,1,0:T(8,128)(2,1)}, u32[]{:S(2)}, u32[]{:S(2)}) collective-permute-start(bf16[1,96,2496]{2,1,0:T(8,128)(2,1)} %dynamic-slice_convert_fusion.2), channel_id=1, source_target_pairs={{0,16},{4,20},{8,24},{12,28},{16,0},{20,4},{24,8},{28,12},{1,17},{... | collective-permute-start | bytes 1437704 | tf_op jit(solution)/shard_map/ppermute | solution.py:507
  619.4 28.5 %collective-permute-start.17 = (f32[96,624]{1,0:T(8,128)}, f32[96,624]{1,0:T(8,128)}, u32[]{:S(2)}, u32[]{:S(2)}) collective-permute-start(f32[96,624]{1,0:T(8,128)} %get-tuple-element.218), channel_id=1, source_target_pairs={{0,1},{1,2},{2,3},{3,0},{4,5},{5,6},{6,7},{7,4},{8,9},{9,10},{10,1... | collective-permute-start | bytes 718856 | tf_op jit(solution)/shard_map/ppermute | solution.py:527
  619.4 28.5 %collective-permute-start.18 = (f32[96,624]{1,0:T(8,128)}, f32[96,624]{1,0:T(8,128)}, u32[]{:S(2)}, u32[]{:S(2)}) collective-permute-start(f32[96,624]{1,0:T(8,128)} %get-tuple-element.220), channel_id=1, source_target_pairs={{0,2},{1,3},{2,0},{3,1},{4,6},{5,7},{6,4},{7,5},{8,10},{9,11},{10,... | collective-permute-start | bytes 718856 | tf_op jit(solution)/shard_map/ppermute | solution.py:527
  621.8 26.1 %collective-permute-start.19 = (f32[96,624]{1,0:T(8,128)}, f32[96,624]{1,0:T(8,128)}, u32[]{:S(2)}, u32[]{:S(2)}) collective-permute-start(f32[96,624]{1,0:T(8,128)} %get-tuple-element.219), channel_id=1, source_target_pairs={{0,3},{1,0},{2,1},{3,2},{4,7},{5,4},{6,5},{7,6},{8,11},{9,8},{10,9... | collective-permute-start | bytes 718856 | tf_op jit(solution)/shard_map/ppermute | solution.py:527
  (37 other events, 378.5 us)
Sparse Core Ops, SparseCore 0:
  22.7 35.4 all-gather.2
  60.7 63.3 all-gather.4
  309.0 113.1 reduce-scatter.1

commit v2 on v0

--- a/solution.py
+++ b/solution.py
@@ -656,7 +656,6 @@
     delta = jnp.sum((grad_context.astype(jnp.float32) * ctx32).reshape(rows, heads, HEAD_DIM), axis=-1)
     delta = delta.T.reshape(heads, rows, 1)
     dk_h, dv_h, dq_h = flash_backward(scaled, key_w, value_w, q_ids, k_ids, lse, delta, grad_context, qlo, qhi, BLOCK, BLOCK, q_steps)
-    early_strip, dq_h, dk_h, dv_h = lax.optimization_barrier((early_strip, dq_h, dk_h, dv_h))
     early_sums = reduce_tensor(early_strip, early_widths, 3)
     g_out_t, g_inner, g_outer_t = early_sums[:3]
     late = early_sums[3:]

time: 631 us -> 685 us (1.086)
  the two profiles are of different devices: /device:TPU:9 before, /device:TPU:4 now
where the time goes in v2:
time: 685 us; the launch traced here: 673 us
  matrix products  132 us (19%)
  Pallas kernels  131 us (19%)
  waiting for transfers between devices  130 us (19%)
  local copies, waits for them, and re-layouts  119 us (17%)
  starting transfers between devices  105 us (15%)
  other arithmetic  41.3 us (6%)
  between operations  14.8 us (2%)
    pallas_call x1, Pallas kernels, flash_backward(): pl.pallas_call(_attn_bwd, grid_spec=grid_spec, cost_estimate=pl.CostEstim...  70.7 us
    ppermute x6, waiting for transfers between devices, reduce_tensor(): lax.ppermute(send, 'tensor', [(s, (s + k) % count) for s in range(count)])  64.9 us
    pallas_call x1, Pallas kernels, flash_forward(): pl.pallas_call(_attn_fwd, grid_spec=grid_spec, cost_estimate=pl.CostEstim...  60.2 us
    ppermute x8, starting transfers between devices, shift_rows(): return lax.ppermute(values, 'tensor', pairs)  59.2 us
    dot_general x6, matrix products, contract_last(): lax.dot_general(left, right, (((1,), (1,)), ((), ())), preferred_element_...  40 us
    ppermute x6, waiting for transfers between devices, cyclic_pieces(): lax.ppermute(piece, 'tensor', [(s, (s + k) % count) for s in range(count)])  36.2 us
    unnamed x82, local copies, waits for them, and re-layouts  29.8 us
    dot_general x1, matrix products, shards(): jnp.dot(hidden_low, wi, preferred_element_type=jnp.float32)  29.7 us
  transfers between devices with their start and end apart: 26, of which 11 were waited for; matrix products, arithmetic and copies ran while one was open for 23% of the time, Pallas kernels for 19%

profile of v2, /device:TPU:4, one launch (start us, length us, event | category | flops | bytes accessed | tf_op | source)
XLA Modules:
  0.0 673.3 jit_solution(4580890666196959477)
XLA Ops:
  15.5 6.9 %collective-permute-done.1 = bf16[96,576]{1,0:T(8,128)(2,1)S(1)} collective-permute-done((bf16[96,576]{1,0:T(8,128)(2,1)S(1)}, bf16[96,576]{1,0:T(8,128)(2,1)S(1)}, u32[]{:S(2)}, u32[]{:S(2)}) %collective-permute-start.1) | collective-permute-done | bytes 110624 | tf_op jit(solution)/shard_map/ppermute | solution.py:451
  29.5 5.6 collective-permute-done.9
  35.2 22.0 %collective-permute-done.8 = bf16[96,1728]{1,0:T(8,128)(2,1)S(1)} collective-permute-done((bf16[96,1728]{1,0:T(8,128)(2,1)S(1)}, bf16[96,1728]{1,0:T(8,128)(2,1)S(1)}, u32[]{:S(2)}, u32[]{:S(2)}) %collective-permute-start.8) | collective-permute-done | bytes 331808 | tf_op jit(solution)/shard_map/ppermute | solution.py:451
  65.4 5.8 collective-permute-start.3
  86.3 9.4 %collective-permute-done.3 = bf16[256,768]{1,0:T(8,128)(2,1)} collective-permute-done((bf16[256,768]{1,0:T(8,128)(2,1)}, bf16[256,768]{1,0:T(8,128)(2,1)}, u32[]{:S(2)}, u32[]{:S(2)}) %collective-permute-start.3) | collective-permute-done | bytes 393248 | tf_op jit(solution)/shard_map/ppermute | solution.py:549
  103.3 6.8 %collective-permute-done.6 = bf16[256,768]{1,0:T(8,128)(2,1)S(1)} collective-permute-done((bf16[256,768]{1,0:T(8,128)(2,1)}, bf16[256,768]{1,0:T(8,128)(2,1)S(1)}, u32[]{:S(2)}, u32[]{:S(2)}) %collective-permute-start.6) | collective-permute-done | bytes 393248 | tf_op jit(solution)/shard_map/ppermute | solution.py:549
  113.4 8.3 %convolution_convert_fusion.2.k_ref = bf16[2816,768]{1,0:T(8,128)(2,1)} fusion(bf16[2816,768]{1,0:T(8,128)(2,1)} %constant_dynamic-update-slice_fusion, bf16[768,2304]{1,0:T(8,128)(2,1)S(1)} %copy-done.18), kind=kOutput, calls=%fused_computation.23 | convolution fusion | flops 3324051456 | bytes 9830400 | tf_op jit(solution)/shard_map/dot_general | solution.py:617
  121.7 7.9 %add_convert_fusion.1.v_ref = bf16[2816,768]{1,0:T(8,128)(2,1)} fusion(bf16[2816,768]{1,0:T(8,128)(2,1)} %constant_dynamic-update-slice_fusion, f32[768]{0:T(1024)S(1)} %convert_element_type.221, bf16[768,2304]{1,0:T(8,128)(2,1)S(1)} %copy-done.18), kind=kOutput, calls=%fused_computation.19 | convolution fusion | flops 3326214144 | bytes 9834496 | tf_op jit(solution)/shard_map/dot_general | solution.py:618
  129.6 60.2 %shard_map.314 = (f32[768,768]{1,0:T(8,128)S(1)}, f32[12,768,1]{2,1,0:T(8,128)}) custom-call(s32[3]{0:T(128)S(1)} %fusion.76.lo_ref, s32[3]{0:T(128)S(1)} %fusion.75.hi_ref, bf16[768,768]{1,0:T(8,128)(2,1)S(1)} %fusion.42.q_ref, bf16[2816,768]{1,0:T(8,128)(2,1)} %convolution_convert_fusion.2.k_ref, bf16[2816,768]{1,0:T(8,128)(2,1)} %add_convert_fusion.1.v_ref, ...), custom_call_target="tpu_custom_call" | custom-call | flops 4831838208 | bytes 19660800 | tf_op jit(solution)/shard_map/pallas_call | solution.py:275
  193.0 29.7 %multiply_convert_fusion = (bf16[768,3072]{1,0:T(8,128)(2,1)S(1)}, f32[768,3072]{1,0:T(8,128)}, f32[768,3072]{1,0:T(8,128)}) fusion(f32[3072]{0:T(1024)S(1)} %convert_element_type.229, bf16[768,6912]{1,0:T(8,128)(2,1)} %all-gather.5.cloned.1.call-done, f32[768,768]{0,1:T(8,128)S(1)} %get-tuple-element.271, f32[768]{0:T(1024)S(1)} %convert_element_type.227, ...), kind=kOutput, calls=%fused_computation.5 | convolution fusion | flops 3782541312 | bytes 30695424 | tf_op jit(solution)/shard_map/dot_general | solution.py:625
  222.6 6.0 fusion.102
  234.2 5.5 convolution_convert_fusion
  239.7 13.7 %fusion.103 = (bf16[3072]{0:T(1024)(128)(2,1)}, bf16[768,3072]{1,0:T(8,128)(2,1)S(1)}) fusion(f32[768,3072]{1,0:T(8,128)} %get-tuple-element.142, bf16[768,768]{0,1:T(8,128)(2,1)S(1)} %get-tuple-element.138, bf16[768,6912]{1,0:T(8,128)(2,1)} %all-gather.5.cloned.1.call-done, f32[768,3072]{1,0:T(8,128)} %get-tuple-element.272, ...), kind=kOutput, calls=%fused_computation.250 | convolution fusion | flops 3661624320 | bytes 29509632 | tf_op jit(solution)/shard_map/dot_general | solution.py:634
  253.4 5.8 convolution_convert_fusion.1
  259.2 7.9 %multiply_reduce_fusion = (bf16[768]{0:T(1024)(128)(2,1)}, f32[768]{0:T(1024)S(1)}, f32[768]{0:T(1024)S(1)}, bf16[768]{0:T(1024)(128)(2,1)}, f32[768,768]{0,1:T(8,128)S(1)}) fusion(f32[768,768]{0,1:T(8,128)S(1)} %get-tuple-element.271, f32[768]{0:T(1024)S(1)} %add_rsqrt_fusion.1, f32[768]{0:T(1024)S(1)} %broadcast_multiply_fusion.5, ...), kind=kOutput, calls=%fused_computation.50 | convolution fusion | flops 3634492416 | bytes 17728512 | tf_op jit(solution)/shard_map/dot_general | solution.py:424
  284.1 18.3 %concatenate.61 = bf16[768,7872]{1,0:T(8,128)(2,1)} concatenate(bf16[768,768]{1,0:T(8,128)(2,1)S(1)} %copy.121, bf16[768,3072]{1,0:T(8,128)(2,1)} %convolution_convert_fusion.1, bf16[768,3072]{1,0:T(8,128)(2,1)} %convolution_convert_fusion, bf16[768,96]{1,0:T(8,128)(2,1)} %bitcast.190, bf16[768,384]{1,0:T(8,128)(2,1)} %bitcast.182, bf16[768,96]{1,0:T(8,128)(2,1)} %bitcast.191, ...), dimensions={1} | concatenate | bytes 24182784 | tf_op jit(solution)/shard_map/concatenate | solution.py:487
  317.8 70.7 %shard_map.315 = (f32[2816,768]{1,0:T(8,128)}, f32[2816,768]{1,0:T(8,128)}, f32[768,768]{1,0:T(8,128)S(1)}) custom-call(s32[11]{0:T(128)S(1)} %copy-done.2, s32[11]{0:T(128)S(1)} %get-tuple-element.135.hi_ref, bf16[768,768]{1,0:T(8,128)(2,1)S(1)} %copy-done.4, bf16[2816,768]{1,0:T(8,128)(2,1)} %convolution_convert_fusion.2.k_ref, ...), custom_call_target="tpu_custom_call" | custom-call | flops 12079595520 | bytes 39321600 | tf_op jit(solution)/shard_map/pallas_call | solution.py:374
  392.1 6.3 fusion.38
  399.5 5.9 convolution_convert_fusion.3
  407.5 4.0 convert_reduce_fusion.2
  412.4 6.5 concatenate.67
  428.3 7.0 %fusion.29 = f32[2816,768]{0,1:T(8,128)S(1)} fusion(f32[2816,768]{1,0:T(8,128)} %get-tuple-element.31, bf16[768,2304]{1,0:T(8,128)(2,1)} %all-gather.3.cloned.1.call-done), kind=kOutput, calls=%fused_computation.64 | convolution fusion | flops 3324051456 | bytes 18481152 | tf_op jit(solution)/shard_map/dot_general | solution.py:424
  439.3 20.8 %collective-permute-start.15 = (bf16[2,96,2496]{2,1,0:T(8,128)(2,1)S(1)}, bf16[2,96,2496]{2,1,0:T(8,128)(2,1)S(1)}, u32[]{:S(2)}, u32[]{:S(2)}) collective-permute-start(bf16[2,96,2496]{2,1,0:T(8,128)(2,1)S(1)} %fusion.54), channel_id=1, source_target_pairs={{0,8},{4,12},{8,0},{12,4},{16,24},{20,28},{24,16},{28,20},{1,9},{5... | collective-permute-start | bytes 2875400 | tf_op jit(solution)/shard_map/ppermute | solution.py:507
  460.1 10.8 %fusion.104 = (bf16[2816,768]{0,1:T(8,128)(2,1)S(1)}, f32[2816,768]{0,1:T(8,128)}) fusion(f32[2816,768]{0,1:T(8,128)S(1)} %fusion.29, bf16[768,2304]{1,0:T(8,128)(2,1)} %all-gather.3.cloned.1.call-done, f32[2816,768]{1,0:T(8,128)} %get-tuple-element.32), kind=kOutput, calls=%fused_computation.251 | convolution fusion | flops 3328376832 | bytes 31457280 | tf_op jit(solution)/shard_map/dot_general | solution.py:424
  470.9 11.5 %collective-permute-done.15 = bf16[2,96,2496]{2,1,0:T(8,128)(2,1)S(1)} collective-permute-done((bf16[2,96,2496]{2,1,0:T(8,128)(2,1)S(1)}, bf16[2,96,2496]{2,1,0:T(8,128)(2,1)S(1)}, u32[]{:S(2)}, u32[]{:S(2)}) %collective-permute-start.15) | collective-permute-done | bytes 958496 | tf_op jit(solution)/shard_map/ppermute | solution.py:507
  486.0 41.8 %collective-permute-start.12 = (bf16[768,768]{0,1:T(8,128)(2,1)}, bf16[768,768]{0,1:T(8,128)(2,1)}, u32[]{:S(2)}, u32[]{:S(2)}) collective-permute-start(bf16[768,768]{0,1:T(8,128)(2,1)} %get-tuple-element.153), channel_id=1, source_target_pairs={{0,1},{1,2},{2,3},{4,5},{5,6},{6,7},{8,9},{9,10},{10,11},{12,13},{... | collective-permute-start | bytes 3538952 | tf_op jit(solution)/shard_map/ppermute | solution.py:549
  530.0 3.8 collective-permute-start.13
  545.2 4.6 collective-permute-start.19
  574.2 9.2 %collective-permute-start.17 = (f32[96,624]{1,0:T(8,128)}, f32[96,624]{1,0:T(8,128)}, u32[]{:S(2)}, u32[]{:S(2)}) collective-permute-start(f32[96,624]{1,0:T(8,128)} %get-tuple-element.212), channel_id=1, source_target_pairs={{0,1},{1,2},{2,3},{3,0},{4,5},{5,6},{6,7},{7,4},{8,9},{9,10},{10,1... | collective-permute-start | bytes 718856 | tf_op jit(solution)/shard_map/ppermute | solution.py:527
  585.5 5.6 fusion.26
  597.8 9.5 %collective-permute-done.22 = f32[96,1968]{1,0:T(8,128)} collective-permute-done((f32[96,1968]{1,0:T(8,128)}, f32[96,1968]{1,0:T(8,128)}, u32[]{:S(2)}, u32[]{:S(2)}) %collective-permute-start.22) | collective-permute-done | bytes 755744 | tf_op jit(solution)/shard_map/ppermute | solution.py:527
  607.3 54.2 %collective-permute-done.21 = f32[96,1968]{1,0:T(8,128)} collective-permute-done((f32[96,1968]{1,0:T(8,128)}, f32[96,1968]{1,0:T(8,128)}, u32[]{:S(2)}, u32[]{:S(2)}) %collective-permute-start.21) | collective-permute-done | bytes 755744 | tf_op jit(solution)/shard_map/ppermute | solution.py:527
  (255 shorter events, 166.5 us)
Async XLA Ops:
  7.2 103.7 %all-gather.3.cloned.1.call-start = ((), (), s32[]{:S(2)}) async-start(), calls=%async_computation.1 | async-start | bytes 3981312 | tf_op jit(solution)/shard_map/all_gather | solution.py:466
  8.2 7.4 %collective-permute-start.2 = (bf16[96,576]{1,0:T(8,128)(2,1)S(1)}, bf16[96,576]{1,0:T(8,128)(2,1)S(1)}, u32[]{:S(2)}, u32[]{:S(2)}) collective-permute-start(bf16[96,576]{1,0:T(8,128)(2,1)S(1)} %pad_maximum_fusion.4), channel_id=1, source_target_pairs={{0,3},{1,0},{2,1},{3,2},{4,7},{5,4},{6,5},{7,6},{8,11},{9,8},{10,9... | collective-permute-start | bytes 331784 | tf_op jit(solution)/shard_map/ppermute | solution.py:451
  11.8 10.6 %collective-permute-start.1 = (bf16[96,576]{1,0:T(8,128)(2,1)S(1)}, bf16[96,576]{1,0:T(8,128)(2,1)S(1)}, u32[]{:S(2)}, u32[]{:S(2)}) collective-permute-start(bf16[96,576]{1,0:T(8,128)(2,1)S(1)} %pad_maximum_fusion.4), channel_id=1, source_target_pairs={{0,2},{1,3},{2,0},{3,1},{4,6},{5,7},{6,4},{7,5},{8,10},{9,11},{10,... | collective-permute-start | bytes 331784 | tf_op jit(solution)/shard_map/ppermute | solution.py:451
  11.8 10.6 %collective-permute-start = (bf16[96,576]{1,0:T(8,128)(2,1)S(1)}, bf16[96,576]{1,0:T(8,128)(2,1)S(1)}, u32[]{:S(2)}, u32[]{:S(2)}) collective-permute-start(bf16[96,576]{1,0:T(8,128)(2,1)S(1)} %pad_maximum_fusion.4), channel_id=1, source_target_pairs={{0,1},{1,2},{2,3},{3,0},{4,5},{5,6},{6,7},{7,4},{8,9},{9,10},{10,1... | collective-permute-start | bytes 331784 | tf_op jit(solution)/shard_map/ppermute | solution.py:451
  24.5 165.4 %all-gather.5.cloned.1.call-start = ((), (), s32[]{:S(2)}) async-start(), calls=%async_computation.2 | async-start | bytes 11943936 | tf_op jit(solution)/shard_map/all_gather | solution.py:466
  24.9 10.2 %collective-permute-start.9 = (bf16[96,1728]{1,0:T(8,128)(2,1)S(1)}, bf16[96,1728]{1,0:T(8,128)(2,1)S(1)}, u32[]{:S(2)}, u32[]{:S(2)}) collective-permute-start(bf16[96,1728]{1,0:T(8,128)(2,1)S(1)} %concatenate.59), channel_id=1, source_target_pairs={{0,3},{1,0},{2,1},{3,2},{4,7},{5,4},{6,5},{7,6},{8,11},{9,8},{10,9... | collective-permute-start | bytes 995336 | tf_op jit(solution)/shard_map/ppermute | solution.py:451
  26.6 30.5 %collective-permute-start.8 = (bf16[96,1728]{1,0:T(8,128)(2,1)S(1)}, bf16[96,1728]{1,0:T(8,128)(2,1)S(1)}, u32[]{:S(2)}, u32[]{:S(2)}) collective-permute-start(bf16[96,1728]{1,0:T(8,128)(2,1)S(1)} %concatenate.59), channel_id=1, source_target_pairs={{0,2},{1,3},{2,0},{3,1},{4,6},{5,7},{6,4},{7,5},{8,10},{9,11},{10,... | collective-permute-start | bytes 995336 | tf_op jit(solution)/shard_map/ppermute | solution.py:451
  27.6 29.6 %collective-permute-start.7 = (bf16[96,1728]{1,0:T(8,128)(2,1)S(1)}, bf16[96,1728]{1,0:T(8,128)(2,1)S(1)}, u32[]{:S(2)}, u32[]{:S(2)}) collective-permute-start(bf16[96,1728]{1,0:T(8,128)(2,1)S(1)} %concatenate.59), channel_id=1, source_target_pairs={{0,1},{1,2},{2,3},{3,0},{4,5},{5,6},{6,7},{7,4},{8,9},{9,10},{10,1... | collective-permute-start | bytes 995336 | tf_op jit(solution)/shard_map/ppermute | solution.py:451
  58.8 14.1 %copy-start.32 = (s32[40]{0:T(128)S(1)}, s32[40]{0:T(128)}, u32[]{:S(2)}) copy-start(s32[40]{0:T(128)} %param.26) | copy-start | bytes 484
  60.6 22.9 %copy-start.16 = (bf16[768,768]{1,0:T(8,128)(2,1)S(1)}, bf16[768,768]{1,0:T(8,128)(2,1)}, u32[]{:S(2)}) copy-start(bf16[768,768]{1,0:T(8,128)(2,1)} %param.43) | copy-start | bytes 3538948
  60.6 489.2 %reduce-scatter.2.cloned.1.call-start = ((), (), s32[]{:S(2)}) async-start(), calls=%async_computation.3 | async-start | bytes 13713408 | tf_op jit(solution)/shard_map/reduce_scatter | solution.py:492
  60.7 36.8 %collective-permute-start.4 = (bf16[768,768]{1,0:T(8,128)(2,1)S(1)}, bf16[768,768]{1,0:T(8,128)(2,1)}, u32[]{:S(2)}, u32[]{:S(2)}) collective-permute-start(bf16[768,768]{1,0:T(8,128)(2,1)S(1)} %copy-done.14), channel_id=1, source_target_pairs={{0,1},{1,2},{2,3},{4,5},{5,6},{6,7},{8,9},{9,10},{10,11},{12,13},{... | collective-permute-start | bytes 3538952 | tf_op jit(solution)/shard_map/ppermute | solution.py:549
  63.1 37.8 %collective-permute-start.5 = (bf16[768,768]{1,0:T(8,128)(2,1)S(1)}, bf16[768,768]{1,0:T(8,128)(2,1)}, u32[]{:S(2)}, u32[]{:S(2)}) collective-permute-start(bf16[768,768]{1,0:T(8,128)(2,1)S(1)} %copy-done.14), channel_id=1, source_target_pairs={{1,0},{2,1},{3,2},{5,4},{6,5},{7,6},{9,8},{10,9},{11,10},{13,12},{... | collective-permute-start | bytes 3538952 | tf_op jit(solution)/shard_map/ppermute | solution.py:549
  65.4 30.3 %collective-permute-start.3 = (bf16[256,768]{1,0:T(8,128)(2,1)}, bf16[256,768]{1,0:T(8,128)(2,1)}, u32[]{:S(2)}, u32[]{:S(2)}) collective-permute-start(bf16[256,768]{1,0:T(8,128)(2,1)} %get-tuple-element.211), channel_id=1, source_target_pairs={{0,2},{1,3},{4,6},{5,7},{8,10},{9,11},{12,14},{13,15},{16,18},{17,... | collective-permute-start | bytes 1179656 | tf_op jit(solution)/shard_map/ppermute | solution.py:549
  71.2 38.9 %collective-permute-start.6 = (bf16[256,768]{1,0:T(8,128)(2,1)}, bf16[256,768]{1,0:T(8,128)(2,1)S(1)}, u32[]{:S(2)}, u32[]{:S(2)}) collective-permute-start(bf16[256,768]{1,0:T(8,128)(2,1)} %get-tuple-element.210), channel_id=1, source_target_pairs={{2,0},{3,1},{6,4},{7,5},{10,8},{11,9},{14,12},{15,13},{18,16},{19,... | collective-permute-start | bytes 1179656 | tf_op jit(solution)/shard_map/ppermute | solution.py:549
  85.2 44.5 %copy-start = (s32[768,1]{1,0:T(8,128)}, s32[768,1]{1,0:T(8,128)S(1)}, u32[]{:S(2)}) copy-start(s32[768,1]{1,0:T(8,128)S(1)} %reshape.539.qs_ref) | copy-start | bytes 9220
  113.4 16.2 %copy-start.3 = (bf16[768,768]{1,0:T(8,128)(2,1)}, bf16[768,768]{1,0:T(8,128)(2,1)S(1)}, u32[]{:S(2)}) copy-start(bf16[768,768]{1,0:T(8,128)(2,1)S(1)} %fusion.42.q_ref) | copy-start | bytes 3538948
  317.8 70.7 %copy-start.15 = (bf16[768,768]{1,0:T(8,128)(2,1)S(1)}, bf16[768,768]{1,0:T(8,128)(2,1)}, u32[]{:S(2)}) copy-start(bf16[768,768]{1,0:T(8,128)(2,1)} %param.25) | copy-start | bytes 3538948
  426.7 8.5 %collective-permute-start.14 = (bf16[4,96,2496]{2,1,0:T(8,128)(2,1)}, bf16[4,96,2496]{2,1,0:T(8,128)(2,1)}, u32[]{:S(2)}, u32[]{:S(2)}) collective-permute-start(bf16[4,96,2496]{2,1,0:T(8,128)(2,1)} %fusion.32), channel_id=1, source_target_pairs={{0,4},{4,0},{8,12},{12,8},{16,20},{20,16},{24,28},{28,24},{1,5},{5... | collective-permute-start | bytes 5750792 | tf_op jit(solution)/shard_map/ppermute | solution.py:507
  439.3 43.1 %collective-permute-start.15 = (bf16[2,96,2496]{2,1,0:T(8,128)(2,1)S(1)}, bf16[2,96,2496]{2,1,0:T(8,128)(2,1)S(1)}, u32[]{:S(2)}, u32[]{:S(2)}) collective-permute-start(bf16[2,96,2496]{2,1,0:T(8,128)(2,1)S(1)} %fusion.54), channel_id=1, source_target_pairs={{0,8},{4,12},{8,0},{12,4},{16,24},{20,28},{24,16},{28,20},{1,9},{5... | collective-permute-start | bytes 2875400 | tf_op jit(solution)/shard_map/ppermute | solution.py:507
  484.3 50.8 %collective-permute-start.16 = (bf16[1,96,2496]{2,1,0:T(8,128)(2,1)S(1)}, bf16[1,96,2496]{2,1,0:T(8,128)(2,1)S(1)}, u32[]{:S(2)}, u32[]{:S(2)}) collective-permute-start(bf16[1,96,2496]{2,1,0:T(8,128)(2,1)S(1)} %dynamic-slice_convert_fusion.2), channel_id=1, source_target_pairs={{0,16},{4,20},{8,24},{12,28},{16,0},{20,4},{24,8},{28,12},{1,17},{... | collective-permute-start | bytes 1437704 | tf_op jit(solution)/shard_map/ppermute | solution.py:507
  486.0 97.4 %collective-permute-start.12 = (bf16[768,768]{0,1:T(8,128)(2,1)}, bf16[768,768]{0,1:T(8,128)(2,1)}, u32[]{:S(2)}, u32[]{:S(2)}) collective-permute-start(bf16[768,768]{0,1:T(8,128)(2,1)} %get-tuple-element.153), channel_id=1, source_target_pairs={{0,1},{1,2},{2,3},{4,5},{5,6},{6,7},{8,9},{9,10},{10,11},{12,13},{... | collective-permute-start | bytes 3538952 | tf_op jit(solution)/shard_map/ppermute | solution.py:549
  527.8 55.6 %collective-permute-start.10 = (bf16[768,768]{0,1:T(8,128)(2,1)}, bf16[768,768]{0,1:T(8,128)(2,1)}, u32[]{:S(2)}, u32[]{:S(2)}) collective-permute-start(bf16[768,768]{0,1:T(8,128)(2,1)} %get-tuple-element.152), channel_id=1, source_target_pairs={{1,0},{2,1},{3,2},{5,4},{6,5},{7,6},{9,8},{10,9},{11,10},{13,12},{... | collective-permute-start | bytes 3538952 | tf_op jit(solution)/shard_map/ppermute | solution.py:549
  530.0 42.7 %collective-permute-start.13 = (bf16[256,768]{0,1:T(8,128)(2,1)}, bf16[256,768]{0,1:T(8,128)(2,1)}, u32[]{:S(2)}, u32[]{:S(2)}) collective-permute-start(bf16[256,768]{0,1:T(8,128)(2,1)} %get-tuple-element.151), channel_id=1, source_target_pairs={{0,2},{1,3},{4,6},{5,7},{8,10},{9,11},{12,14},{13,15},{16,18},{17,... | collective-permute-start | bytes 1179656 | tf_op jit(solution)/shard_map/ppermute | solution.py:549
  533.8 40.4 %collective-permute-start.11 = (bf16[256,768]{0,1:T(8,128)(2,1)}, bf16[256,768]{0,1:T(8,128)(2,1)}, u32[]{:S(2)}, u32[]{:S(2)}) collective-permute-start(bf16[256,768]{0,1:T(8,128)(2,1)} %get-tuple-element.150), channel_id=1, source_target_pairs={{2,0},{3,1},{6,4},{7,5},{10,8},{11,9},{14,12},{15,13},{18,16},{19,... | collective-permute-start | bytes 1179656 | tf_op jit(solution)/shard_map/ppermute | solution.py:549
  545.2 39.7 %collective-permute-start.19 = (f32[96,624]{1,0:T(8,128)}, f32[96,624]{1,0:T(8,128)}, u32[]{:S(2)}, u32[]{:S(2)}) collective-permute-start(f32[96,624]{1,0:T(8,128)} %get-tuple-element.213), channel_id=1, source_target_pairs={{0,3},{1,0},{2,1},{3,2},{4,7},{5,4},{6,5},{7,6},{8,11},{9,8},{10,9... | collective-permute-start | bytes 718856 | tf_op jit(solution)/shard_map/ppermute | solution.py:527
  570.1 15.4 %copy-start.8 = (f32[768,768]{0,1:T(8,128)S(1)}, f32[768,768]{0,1:T(8,128)}, u32[]{:S(2)}) copy-start(f32[768,768]{0,1:T(8,128)} %copy-done.7) | copy-start | bytes 7077892
  572.7 21.4 %collective-permute-start.18 = (f32[96,624]{1,0:T(8,128)}, f32[96,624]{1,0:T(8,128)}, u32[]{:S(2)}, u32[]{:S(2)}) collective-permute-start(f32[96,624]{1,0:T(8,128)} %get-tuple-element.214), channel_id=1, source_target_pairs={{0,2},{1,3},{2,0},{3,1},{4,6},{5,7},{6,4},{7,5},{8,10},{9,11},{10,... | collective-permute-start | bytes 718856 | tf_op jit(solution)/shard_map/ppermute | solution.py:527
  574.2 21.1 %collective-permute-start.17 = (f32[96,624]{1,0:T(8,128)}, f32[96,624]{1,0:T(8,128)}, u32[]{:S(2)}, u32[]{:S(2)}) collective-permute-start(f32[96,624]{1,0:T(8,128)} %get-tuple-element.212), channel_id=1, source_target_pairs={{0,1},{1,2},{2,3},{3,0},{4,5},{5,6},{6,7},{7,4},{8,9},{9,10},{10,1... | collective-permute-start | bytes 718856 | tf_op jit(solution)/shard_map/ppermute | solution.py:527
  583.4 23.9 %collective-permute-start.22 = (f32[96,1968]{1,0:T(8,128)}, f32[96,1968]{1,0:T(8,128)}, u32[]{:S(2)}, u32[]{:S(2)}) collective-permute-start(f32[96,1968]{1,0:T(8,128)} %get-tuple-element.155), channel_id=1, source_target_pairs={{0,3},{1,0},{2,1},{3,2},{4,7},{5,4},{6,5},{7,6},{8,11},{9,8},{10,9... | collective-permute-start | bytes 2267144 | tf_op jit(solution)/shard_map/ppermute | solution.py:527
  583.4 78.1 %collective-permute-start.21 = (f32[96,1968]{1,0:T(8,128)}, f32[96,1968]{1,0:T(8,128)}, u32[]{:S(2)}, u32[]{:S(2)}) collective-permute-start(f32[96,1968]{1,0:T(8,128)} %get-tuple-element.156), channel_id=1, source_target_pairs={{0,2},{1,3},{2,0},{3,1},{4,6},{5,7},{6,4},{7,5},{8,10},{9,11},{10,... | collective-permute-start | bytes 2267144 | tf_op jit(solution)/shard_map/ppermute | solution.py:527
  584.9 76.6 %collective-permute-start.20 = (f32[96,1968]{1,0:T(8,128)}, f32[96,1968]{1,0:T(8,128)}, u32[]{:S(2)}, u32[]{:S(2)}) collective-permute-start(f32[96,1968]{1,0:T(8,128)} %get-tuple-element.154), channel_id=1, source_target_pairs={{0,1},{1,2},{2,3},{3,0},{4,5},{5,6},{6,7},{7,4},{8,9},{9,10},{10,1... | collective-permute-start | bytes 2267144 | tf_op jit(solution)/shard_map/ppermute | solution.py:527
  (30 other events, 109.9 us)
Sparse Core Ops, SparseCore 0:
  24.6 33.8 all-gather.2
  60.9 63.3 all-gather.4
  305.7 117.1 reduce-scatter.1
